TPU v7x, 128 devices: a whole 4x4x4 slice. The times are simulated.
128 devices in a mesh: gx: 16 (over y_hi, x, core), gy: 8 (over z, y_lo).
Axes of the slice: x: 4, y: 4 (y_hi: 2, y_lo: 2; y = y_hi * 2 + y_lo), z: 4, core: 2. Of those that a mesh axis runs over, the one named last changes fastest.
Arguments:
- fv_state: float32 [4, 128, 128, 1024], P(None, 'gx', 'gy'), may hold values from -6 to 6
- buffer_owner: int32 [131072, 1], P(('gx', 'gy')), may hold values from 0 to 127; in each aligned block of 1024 rows (0 to 1023, 1024 to 2047, ...) at most 16 rows name the same one
- buffer_cell: int32 [131072], P(('gx', 'gy')), may hold values from 0 to 131071
- buffer_frac: float32 [3, 131072], P(None, ('gx', 'gy')), may hold values from 0 to 1
- buffer_count: int32 [128], P(('gx', 'gy')), may hold values from 341 to 1024, as said below
- sph_offset: float32 [3, 64, 32, 128], P(None, 'gx', 'gy'), may hold values from 0 to 1
- sph_vel: float32 [3, 64, 32, 128], P(None, 'gx', 'gy'), may hold values from -6 to 6
- sph_press: float32 [64, 32, 128], P('gx', 'gy'), may hold values from 0.1 to 1
- tile_count: int32 [64, 32], P('gx', 'gy'), may hold values from 64 to 128
Outputs:
- fv_next: float32 [4, 128, 128, 1024], P(None, 'gx', 'gy')
- buffer_state: float32 [4, 131072], P(None, ('gx', 'gy'))
- sph_accel: float32 [3, 64, 32, 128], P(None, 'gx', 'gy')
Inputs may be any that keep to these rules, and one draw needn't show every extreme that they name: `buffer_owner`: among the 1024 rows of one device, no owner is named by more than 16 rows, a bound that some block reaches. `buffer_count`: the live buffer slots of a device are its first ones; some device has 1024 live slots and some has 341. `tile_count`: the live particles of a tile occupy its first slots.
All inputs are finite; a program needn't handle non-finite values.
Results may differ from a plain program's by a relative error of at most 0.0003.
Values sent between devices are 32-bit elements; how exact they have to be, the bound alone decides.
No kernel may reach another device: no remote copies, remote signals or barrier semaphores. Data moves between devices by JAX's collectives and lax.ppermute only.
A program may use at most 256 MiB of HBM per device.

v0:
```python
import jax
import jax.numpy as jnp
from jax import lax
from jax.experimental import pallas as pl
from jax.experimental.pallas import tpu as pltpu
from jax.sharding import PartitionSpec as P


STEP_RATIO = 0.3
VISCOSITY = 0.02
FORCE_SCALE = 0.1


def padded_2(array, sides, width):
    for axis, dim in sides:
        count, length = (lax.axis_size(axis), array.shape[dim])
        up = [(i, (i + 1) % count) for i in range(count - 1)]
        down = [(j, i) for i, j in up]
        last = lax.slice_in_dim(array, length - width, length, axis=dim)
        leading = lax.slice_in_dim(array, 0, width, axis=dim)
        before = lax.ppermute(last, axis, up)
        after = lax.ppermute(leading, axis, down)
        array = jnp.concatenate([before, array, after], axis=dim)
    return array


def from_behind(array, axis, by):
    count = lax.axis_size(axis)
    pairs = [(i, i + by) for i in range(count) if 0 <= i + by < count]
    return lax.ppermute(array, axis, pairs)


def flux_kernel(
    state_ref, x_lo_ref, x_hi_ref, y_lo_ref, y_hi_ref, out_ref, row_ref, column_ref, corner_ref, table_ref
):
    channels, rows, cols, depth = state_ref.shape
    main_rows = channels * rows * cols
    table_ref[main_rows:, :] = jnp.zeros((table_ref.shape[0] - main_rows, depth), jnp.float32)
    col_ids = lax.broadcasted_iota(jnp.int32, (cols, depth), 0)
    lane_ids = lax.broadcasted_iota(jnp.int32, (cols, depth), 1)
    for x in range(rows):
        centre = [state_ref[c, x] for c in range(channels)]
        ahead = [state_ref[c, x + 1] if x + 1 < rows else x_hi_ref[c, 0] for c in range(channels)]
        behind = [state_ref[c, x - 1] if x > 0 else x_lo_ref[c, 0] for c in range(channels)]
        up_y = [
            jnp.where(col_ids == cols - 1, y_hi_ref[c, x], pltpu.roll(centre[c], cols - 1, 0))
            for c in range(channels)
        ]
        down_y = [
            jnp.where(col_ids == 0, y_lo_ref[c, x], pltpu.roll(centre[c], 1, 0))
            for c in range(channels)
        ]
        up_z = [
            jnp.where(lane_ids == depth - 1, 0.0, pltpu.roll(centre[c], depth - 1, 1))
            for c in range(channels)
        ]
        down_z = [jnp.where(lane_ids == 0, 0.0, pltpu.roll(centre[c], 1, 1)) for c in range(channels)]
        change = None
        for normal, (lower, upper) in ((1, (behind, ahead)), (2, (down_y, up_y)), (3, (down_z, up_z))):
            high = face_flux_list(centre, upper, normal)
            low = face_flux_list(lower, centre, normal)
            step = [high[c] - low[c] for c in range(channels)]
            change = step if change is None else [change[c] + step[c] for c in range(channels)]
        for c in range(channels):
            result = centre[c] - STEP_RATIO * change[c]
            out_ref[c, x] = result
            table_ref[(c * rows + x) * cols : (c * rows + x + 1) * cols, :] = result
            column_ref[c, x : x + 1] = result[0:1]
            if x == 0:
                row_ref[c] = result
                corner_ref[c : c + 1] = result[0:1]


def face_flux_list(left_side, right_side, normal):
    fluxes = [-0.5 * (right_side[c] - left_side[c]) for c in range(len(left_side))]
    fluxes[0] = fluxes[0] + 0.5 * (left_side[normal] + right_side[normal])
    fluxes[normal] = fluxes[normal] + 0.5 * (left_side[0] + right_side[0])
    return fluxes


def table_rows(channels, rows, cols):
    used = channels * (rows * cols + rows + cols + 1)
    return -(-used // 128) * 128


def flux_sweep(state, x_lo, x_hi, y_lo, y_hi):
    channels, rows, cols, depth = state.shape
    return pl.pallas_call(
        flux_kernel,
        out_shape=(
            jax.ShapeDtypeStruct(state.shape, state.dtype),
            jax.ShapeDtypeStruct((channels, cols, depth), state.dtype),
            jax.ShapeDtypeStruct((channels, rows, depth), state.dtype),
            jax.ShapeDtypeStruct((channels, depth), state.dtype),
            jax.ShapeDtypeStruct((table_rows(channels, rows, cols), depth), state.dtype),
        ),
    )(state, x_lo, x_hi, y_lo, y_hi)


def from_diagonal(array):
    count_x = lax.axis_size("gx")
    count_y = lax.axis_size("gy")
    pairs = [
        ((i + 1) * count_y + j + 1, i * count_y + j)
        for i in range(count_x - 1)
        for j in range(count_y - 1)
    ]
    return lax.ppermute(array, ("gx", "gy"), pairs)


def answer_requests(table, shape, arrived):
    channels, cells_x, cells_y, cells_z = shape
    count = arrived.shape[1]
    cell_index = arrived[3].astype(jnp.int32)
    base_x = cell_index // (cells_y * cells_z)
    base_y = cell_index // cells_z % cells_y
    base_z = cell_index % cells_z
    frac_x, frac_y, frac_z = arrived[0], arrived[1], arrived[2]
    z_ids = lax.broadcasted_iota(jnp.int32, (cells_z, count), 0)
    z_weight = jnp.where(z_ids == base_z[None, :], 1.0 - frac_z[None, :], 0.0) + jnp.where(
        z_ids == base_z[None, :] + 1, frac_z[None, :], 0.0
    )
    columns = lax.dot_general(
        table,
        z_weight,
        (((1,), (0,)), ((), ())),
        precision=lax.Precision.HIGH,
        preferred_element_type=jnp.float32,
    )
    x_ids = lax.broadcasted_iota(jnp.int32, (cells_x, count), 0)
    y_ids = lax.broadcasted_iota(jnp.int32, (cells_y, count), 0)
    weight_x = jnp.where(x_ids == base_x, 1.0 - frac_x, 0.0) + jnp.where(x_ids == base_x + 1, frac_x, 0.0)
    weight_y = jnp.where(y_ids == base_y, 1.0 - frac_y, 0.0) + jnp.where(y_ids == base_y + 1, frac_y, 0.0)
    edge_x = jnp.where(base_x + 1 == cells_x, frac_x, 0.0)
    edge_y = jnp.where(base_y + 1 == cells_y, frac_y, 0.0)
    weight_main = (weight_x[:, None, :] * weight_y[None, :, :]).reshape(cells_x * cells_y, count)
    weight_extra = jnp.concatenate(
        [edge_x[None] * weight_y, weight_x * edge_y[None], (edge_x * edge_y)[None]], axis=0
    )
    main_rows = cells_x * cells_y
    extra_rows = cells_x + cells_y + 1
    values = []
    for c in range(channels):
        main = columns[c * main_rows : (c + 1) * main_rows]
        start = channels * main_rows + c * extra_rows
        extra = columns[start : start + extra_rows]
        values.append(jnp.sum(main * weight_main, axis=0) + jnp.sum(extra * weight_extra, axis=0))
    return jnp.stack(values)


def pair_sums(own_tiles, other_tiles):
    separations = [own_tiles[c][:, None, :] - other_tiles[c][:, :, None] for c in range(3)]
    distance = jnp.sqrt(sum(separation * separation for separation in separations))
    closeness = jnp.maximum(1.0 - distance, 0.0)
    weight = 20.0 * closeness * closeness * closeness * other_tiles[7][:, :, None]
    push_term = (own_tiles[6][:, None, :] + other_tiles[6][:, :, None]) * weight
    weight_total = jnp.sum(weight, axis=1)
    result = []
    for channel, separation in enumerate(separations):
        drag_term = (
            jnp.sum(weight * other_tiles[3 + channel][:, :, None], axis=1)
            - weight_total * own_tiles[3 + channel]
        )
        result.append(jnp.sum(push_term * separation, axis=1) + VISCOSITY * drag_term)
    return jnp.stack(result)


def pieces(values):
    high = lax.reduce_precision(values, exponent_bits=8, mantissa_bits=7)
    rest = values - high
    middle = lax.reduce_precision(rest, exponent_bits=8, mantissa_bits=7)
    low = rest - middle
    return jnp.concatenate([high, middle, low], axis=0).astype(jnp.bfloat16)


def joined(parts, count):
    return (parts[:count] + parts[count : 2 * count]) + parts[2 * count :]


def step_body(
    fv_state,
    buffer_owner,
    buffer_cell,
    buffer_frac,
    buffer_count,
    sph_offset,
    sph_vel,
    sph_press,
    tile_count,
):
    grid_x = lax.axis_size("gx")
    grid_y = lax.axis_size("gy")
    devices = grid_x * grid_y
    buffer_rows = buffer_cell.shape[0]
    capacity = 2 * buffer_rows // devices
    slot_total = devices * capacity
    owner_ids = buffer_owner[:, 0]
    row_ids = jnp.arange(buffer_rows, dtype=jnp.int32)
    is_live = row_ids < buffer_count[0]
    one_hot = (owner_ids[:, None] == jnp.arange(devices, dtype=jnp.int32)[None, :]) & is_live[
        :, None
    ]
    one_hot_float = one_hot.astype(jnp.bfloat16)
    lower_mask = (row_ids[None, :] < row_ids[:, None]).astype(jnp.bfloat16)
    earlier = jnp.dot(lower_mask, one_hot_float, preferred_element_type=jnp.float32)
    ranks = jnp.sum(jnp.where(one_hot, earlier, 0.0), axis=1).astype(jnp.int32)
    target = jnp.where(is_live, owner_ids * capacity + ranks, slot_total)
    selector = (target[:, None] == jnp.arange(slot_total, dtype=jnp.int32)[None, :]).astype(
        jnp.bfloat16
    )
    request = jnp.concatenate([buffer_frac, buffer_cell[None].astype(jnp.float32)], axis=0)
    outgoing = joined(
        jnp.dot(pieces(request), selector, preferred_element_type=jnp.float32), request.shape[0]
    )
    arrived = lax.all_to_all(outgoing, ("gx", "gy"), split_axis=1, concat_axis=1, tiled=True)
    fv_state, arrived = lax.optimization_barrier((fv_state, arrived))
    x_lo = from_behind(fv_state[:, -1:], "gx", 1)
    x_hi = from_behind(fv_state[:, :1], "gx", -1)
    y_lo = from_behind(fv_state[:, :, -1:], "gy", 1)
    y_hi = from_behind(fv_state[:, :, :1], "gy", -1)
    fv_next, first_row, first_column, first_corner, table = flux_sweep(
        fv_state, x_lo, x_hi, y_lo, y_hi
    )
    row_next = from_behind(first_row, "gx", -1)
    column_next = from_behind(first_column, "gy", -1)
    corner_next = from_diagonal(first_corner)
    extra = jnp.concatenate([row_next, column_next, corner_next[:, None]], axis=1)
    table = lax.dynamic_update_slice(
        table, extra.reshape(-1, extra.shape[-1]), (fv_next.size // fv_next.shape[-1], 0)
    )
    returned = lax.all_to_all(
        answer_requests(table, fv_next.shape, arrived), ("gx", "gy"), split_axis=1, concat_axis=1, tiled=True
    )
    picked = joined(
        lax.dot_general(
            pieces(returned),
            selector,
            (((1,), (1,)), ((), ())),
            preferred_element_type=jnp.float32,
        ),
        returned.shape[0],
    )
    buffer_state = jnp.where(is_live[None, :], picked, 0.0)
    tiles_x, tiles_y, tile_slots = sph_press.shape
    tile_live = (
        jnp.arange(tile_slots, dtype=jnp.int32)[None, None, :] < tile_count[:, :, None]
    ).astype(jnp.float32)
    packed = jnp.concatenate([sph_offset, sph_vel, sph_press[None], tile_live[None]], axis=0)
    framed = padded_2(packed, (("gx", 1), ("gy", 2)), 1)
    own_tiles = packed.reshape(8, tiles_x * tiles_y, tile_slots)
    neighbours = []
    for corner in range(9):
        step_x = corner // 3 - 1
        step_y = corner % 3 - 1
        window = framed[:, 1 + step_x : 1 + step_x + tiles_x, 1 + step_y : 1 + step_y + tiles_y]
        shift = jnp.array([step_x, step_y, 0, 0, 0, 0, 0, 0], jnp.float32)[:, None, None, None]
        neighbours.append(window + shift)
    other_tiles = jnp.stack(neighbours, axis=3).reshape(8, tiles_x * tiles_y, 9 * tile_slots)
    total = pair_sums(own_tiles, other_tiles)
    sph_accel = (FORCE_SCALE * total * own_tiles[7][None]).reshape(3, tiles_x, tiles_y, tile_slots)
    return (fv_next, buffer_state, sph_accel)


def solution(mesh):
    return sharded(mesh)


def sharded(mesh):
    return jax.shard_map(
        step_body,
        mesh=mesh,
        in_specs=(
            P(None, "gx", "gy", None),
            P(("gx", "gy"), None),
            P(("gx", "gy")),
            P(None, ("gx", "gy")),
            P(("gx", "gy")),
            P(None, "gx", "gy", None),
            P(None, "gx", "gy", None),
            P("gx", "gy", None),
            P("gx", "gy"),
        ),
        out_specs=(P(None, "gx", "gy", None), P(None, ("gx", "gy")), P(None, "gx", "gy", None)),
        check_vma=False,
    )
```

profile of v0, /device:TPU:1, one launch (start us, length us, event | category | flops | bytes accessed | tf_op | source)
XLA Modules:
  0.0 140.0 jit_solution(13754616256982653732)
XLA Ops:
  1.4 1.4 fusion.25
  2.9 0.7 convert_element_type.54
  3.6 0.7 compare_select_fusion.4
  4.3 0.7 reduce-precision_convert_fusion.3
  5.0 1.6 %fusion.14 = f32[12,2048]{1,0:T(8,128)S(1)} fusion(s32[1024]{0:T(1024)S(1)} %bitcast.156, bf16[4,1024]{1,0:T(4,128)(2,1)S(1)} %get-tuple-element.86, bf16[4,1024]{1,0:T(4,128)(2,1)S(1)} %get-tuple-element.85, bf16[4,1024]{1,0:T(4,128)(2,1)S(1)} %get-tuple-element.84), kind=kOutput, calls=%fused_computation.28 | convolution fusion | flops 52502528 | bytes 126976 | tf_op jit(solution)/shard_map/dot_general | solution.py:213
  6.6 0.1 all_to_all.14
  6.7 0.9 copy.54
  7.6 11.5 %all-to-all-start = ((f32[4,128,16]{2,0,1:T(4,128)}), f32[4,128,16]{2,0,1:T(4,128)S(1)}, u32[]{:S(2)}, u32[]{:S(2)}) async-start(f32[4,128,16]{2,0,1:T(4,128)} %copy.54), calls=%async_computation | async-start | bytes 524288 | tf_op jit(solution)/shard_map/all_to_all | solution.py:215
  19.2 3.0 %collective-permute-start.8 = (f32[8,1,4,128]{3,2,1,0:T(4,128)S(1)}, f32[8,1,4,128]{3,2,1,0:T(4,128)S(1)}, u32[]{:S(2)}, u32[]{:S(2)}) collective-permute-start(f32[8,1,4,128]{3,2,1,0:T(4,128)S(1)} %get-tuple-element.60), channel_id=1, source_target_pairs={{8,0},{16,8},{24,16},{32,24},{40,32},{48,40},{56,48},{64,56},{72,6... | collective-permute-start | bytes 49160 | tf_op jit(solution)/shard_map/ppermute | solution.py:22
  22.2 2.6 %collective-permute-start.7 = (f32[8,1,4,128]{3,2,1,0:T(4,128)S(1)}, f32[8,1,4,128]{3,2,1,0:T(4,128)S(1)}, u32[]{:S(2)}, u32[]{:S(2)}) collective-permute-start(f32[8,1,4,128]{3,2,1,0:T(4,128)S(1)} %get-tuple-element.59), channel_id=1, source_target_pairs={{0,8},{8,16},{16,24},{24,32},{32,40},{40,48},{48,56},{56,64},{64,7... | collective-permute-start | bytes 49160 | tf_op jit(solution)/shard_map/ppermute | solution.py:21
  24.9 0.8 collective-permute-done.7
  25.7 1.3 collective-permute-start.10
  27.0 4.0 %collective-permute-start.9 = (f32[8,6,1,128]{3,2,1,0:T(1,128)S(1)}, f32[8,6,1,128]{3,2,1,0:T(1,128)S(1)}, u32[]{:S(2)}, u32[]{:S(2)}) collective-permute-start(f32[8,6,1,128]{3,2,1,0:T(1,128)S(1)} %get-tuple-element.58), channel_id=1, source_target_pairs={{0,1},{1,2},{2,3},{3,4},{4,5},{5,6},{6,7},{8,9},{9,10},{10,11},{11... | collective-permute-start | bytes 73736 | tf_op jit(solution)/shard_map/ppermute | solution.py:21
  31.0 0.2 all_to_all.16
  31.2 1.1 fusion.78
  32.3 1.8 %fusion.77 = (f32[4,8,1,1024]{3,2,1,0:T(1,128)S(1)}, f32[4,8,1,1024]{3,2,1,0:T(1,128)S(1)}) fusion(f32[4,8,16,1024]{3,2,1,0:T(8,128)} %state_ref), kind=kLoop, calls=%fused_computation.189 | loop fusion | bytes 524288 | tf_op jit(solution)/shard_map/slice | solution.py:220
  34.0 4.8 %collective-permute-start = (f32[4,1,16,1024]{3,2,1,0:T(8,128)S(1)}, f32[4,1,16,1024]{3,2,1,0:T(8,128)S(1)}, u32[]{:S(2)}, u32[]{:S(2)}) collective-permute-start(f32[4,1,16,1024]{3,2,1,0:T(8,128)S(1)} %get-tuple-element.46), channel_id=1, source_target_pairs={{0,8},{8,16},{16,24},{24,32},{32,40},{40,48},{48,56},{56,64},{64,7... | collective-permute-start | bytes 786440 | tf_op jit(solution)/shard_map/ppermute | solution.py:30
  38.8 1.9 %collective-permute-start.1 = (f32[4,1,16,1024]{3,2,1,0:T(8,128)S(1)}, f32[4,1,16,1024]{3,2,1,0:T(8,128)S(1)}, u32[]{:S(2)}, u32[]{:S(2)}) collective-permute-start(f32[4,1,16,1024]{3,2,1,0:T(8,128)S(1)} %get-tuple-element.45), channel_id=1, source_target_pairs={{8,0},{16,8},{24,16},{32,24},{40,32},{48,40},{56,48},{64,56},{72,6... | collective-permute-start | bytes 786440 | tf_op jit(solution)/shard_map/ppermute | solution.py:30
  40.7 4.2 %collective-permute-start.2 = (f32[4,8,1,1024]{3,2,1,0:T(1,128)S(1)}, f32[4,8,1,1024]{3,2,1,0:T(1,128)S(1)}, u32[]{:S(2)}, u32[]{:S(2)}) collective-permute-start(f32[4,8,1,1024]{3,2,1,0:T(1,128)S(1)} %get-tuple-element.44), channel_id=1, source_target_pairs={{0,1},{1,2},{2,3},{3,4},{4,5},{5,6},{6,7},{8,9},{9,10},{10,11},{11... | collective-permute-start | bytes 393224 | tf_op jit(solution)/shard_map/ppermute | solution.py:30
  44.9 0.1 fusion.80
  45.2 0.1 broadcast_multiply_fusion
  45.3 1.3 collective-permute-start.3
  46.8 0.1 fusion.53
  47.2 0.1 fusion.46
  47.4 0.1 fusion.42
  47.5 0.1 fusion.39
  48.2 2.9 %collective-permute-done.3.y_hi_ref = f32[4,8,1,1024]{3,2,1,0:T(1,128)S(1)} collective-permute-done((f32[4,8,1,1024]{3,2,1,0:T(1,128)S(1)}, f32[4,8,1,1024]{3,2,1,0:T(1,128)S(1)}, u32[]{:S(2)}, u32[]{:S(2)}) %collective-permute-start.3) | collective-permute-done | bytes 131104 | tf_op jit(solution)/shard_map/ppermute | solution.py:30
  51.1 0.6 copy-done.6
  51.7 0.1 copy-done.3
  51.8 0.7 copy-done.4
  52.5 6.7 %shard_map.193 = (f32[4,8,16,1024]{3,2,1,0:T(8,128)}, f32[4,16,1024]{2,1,0:T(8,128)}, f32[4,8,1024]{2,1,0:T(8,128)}, f32[4,1024]{1,0:T(4,128)}, f32[640,1024]{1,0:T(8,128)}) custom-call(f32[4,8,16,1024]{3,2,1,0:T(8,128)} %state_ref, f32[4,1,16,1024]{3,2,1,0:T(8,128)} %copy-done.3, f32[4,1,16,1024]{3,2,1,0:T(8,128)} %copy-done.4, ...), custom_call_target="tpu_custom_call" | custom-call | tf_op jit(solution)/shard_map/pallas_call | solution.py:88
  59.2 1.9 %collective-permute-start.4 = (f32[4,16,1024]{2,1,0:T(8,128)}, f32[4,16,1024]{2,1,0:T(8,128)S(1)}, u32[]{:S(2)}, u32[]{:S(2)}) collective-permute-start(f32[4,16,1024]{2,1,0:T(8,128)} %get-tuple-element.13), channel_id=1, source_target_pairs={{8,0},{16,8},{24,16},{32,24},{40,32},{48,40},{56,48},{64,56},{72,6... | collective-permute-start | bytes 786440 | tf_op jit(solution)/shard_map/ppermute | solution.py:30
  61.1 20.8 %multiply_reduce_fusion.2 = (f32[16,128]{1,0:T(8,128)S(1)}, f32[16,128]{1,0:T(8,128)S(1)}, f32[16,128]{1,0:T(8,128)S(1)}, f32[16,128]{1,0:T(8,128)S(1)}, f32[16,...) fusion(f32[16,1152]{1,0:T(8,128)S(1)} %get-tuple-element.93, f32[16,1152]{1,0:T(8,128)S(1)} %get-tuple-element.94, ...), kind=kLoop, calls=%fused_computation.18 | loop fusion | flops 68405248 | bytes 679936 | tf_op jit(solution)/shard_map/reduce_sum | solution.py:161
  81.9 1.3 collective-permute-start.6
  83.2 1.5 %collective-permute-start.5 = (f32[4,8,1024]{2,1,0:T(8,128)}, f32[4,8,1024]{2,1,0:T(8,128)S(1)}, u32[]{:S(2)}, u32[]{:S(2)}) collective-permute-start(f32[4,8,1024]{2,1,0:T(8,128)} %get-tuple-element.14), channel_id=1, source_target_pairs={{1,0},{2,1},{3,2},{4,3},{5,4},{6,5},{7,6},{9,8},{10,9},{11,10},{12... | collective-permute-start | bytes 393224 | tf_op jit(solution)/shard_map/ppermute | solution.py:30
  84.7 6.6 %collective-permute-done.6 = f32[4,1024]{1,0:T(4,128)S(1)} collective-permute-done((f32[4,1024]{1,0:T(4,128)}, f32[4,1024]{1,0:T(4,128)S(1)}, u32[]{:S(2)}, u32[]{:S(2)}) %collective-permute-start.6) | collective-permute-done | bytes 16416 | tf_op jit(solution)/shard_map/ppermute | solution.py:108
  91.3 1.4 collective-permute-done.5
  92.8 1.8 %dynamic_update_slice.3 = f32[640,1024]{1,0:T(8,128)} dynamic-update-slice(f32[640,1024]{1,0:T(8,128)} %get-tuple-element.12, f32[100,1024]{1,0:T(8,128)S(1)} %reshape.428, s32[]{:T(128)} %constant.78.clone.1, s32[]{:T(128)} %constant.79.clone.1) | dynamic-update-slice | bytes 819204 | tf_op jit(solution)/shard_map/dynamic_update_slice | solution.py:228
  94.7 10.7 %fusion.9 = f32[640,2048]{1,0:T(8,128)S(1)} fusion(f32[640,1024]{1,0:T(8,128)} %dynamic_update_slice.3, f32[2048]{0:T(1024)S(1)} %bitcast.142, s32[2048]{0:T(1024)S(1)} %bitcast.143, f32[2048]{0:T(1024)S(1)} %bitcast.141, s32[2048]{0:T(1024)S(1)} %bitcast.144), kind=kOutput, calls=%fused_computation.20 | convolution fusion | flops 8063549440 | bytes 7897088 | tf_op jit(solution)/shard_map/dot_general | solution.py:123
  105.4 0.6 fusion.29
  106.0 0.2 fusion.35
  106.6 0.9 copy.57
  107.5 19.5 %all-to-all-start.1 = ((f32[4,128,16]{2,0,1:T(4,128)}), f32[4,128,16]{2,0,1:T(4,128)S(1)}, u32[]{:S(2)}, u32[]{:S(2)}) async-start(f32[4,128,16]{2,0,1:T(4,128)} %copy.57), calls=%async_computation.1 | async-start | bytes 524288 | tf_op jit(solution)/shard_map/all_to_all | solution.py:231
  126.9 0.6 maximum_multiply_fusion
  127.6 9.9 %all-to-all-done.1 = f32[4,128,16]{2,0,1:T(4,128)S(1)} async-done(((f32[4,128,16]{2,0,1:T(4,128)}), f32[4,128,16]{2,0,1:T(4,128)S(1)}, u32[]{:S(2)}, u32[]{:S(2)}) %all-to-all-start.1) | async-done | bytes 32800 | tf_op jit(solution)/shard_map/all_to_all | solution.py:231
  137.5 0.2 all_to_all.18
  137.6 1.7 %fusion.13 = f32[12,1024]{1,0:T(8,128)S(1)} fusion(s32[1024]{0:T(1024)S(1)} %bitcast.157, bf16[4,2048]{1,0:T(4,128)(2,1)S(1)} %get-tuple-element.65, bf16[4,2048]{1,0:T(4,128)(2,1)S(1)} %get-tuple-element.66, bf16[4,2048]{1,0:T(4,128)(2,1)S(1)} %get-tuple-element.64), kind=kOutput, calls=%fused_computation.27 | convolution fusion | flops 52576256 | bytes 102400 | tf_op jit(solution)/shard_map/dot_general | solution.py:235
  139.3 0.6 fusion.68
  (86 shorter events, 1.9 us)
Async XLA Ops:
  0.6 18.5 %copy-start.7 = (s32[4,4]{1,0:T(4,128)S(1)}, s32[4,4]{1,0:T(4,128)}, u32[]{:S(2)}) copy-start(s32[4,4]{1,0:T(4,128)} %param.26) | copy-start | bytes 196
  0.6 18.5 %copy-start.2 = (f32[4,4,128]{2,1,0:T(4,128)S(1)}, f32[4,4,128]{2,1,0:T(4,128)}, u32[]{:S(2)}) copy-start(f32[4,4,128]{2,1,0:T(4,128)} %param.25) | copy-start | bytes 24580
  0.7 18.5 %copy-start.1 = (f32[3,4,4,128]{3,2,1,0:T(4,128)S(1)}, f32[3,4,4,128]{3,2,1,0:T(4,128)}, u32[]{:S(2)}) copy-start(f32[3,4,4,128]{3,2,1,0:T(4,128)} %param.24) | copy-start | bytes 73732
  0.7 18.5 %copy-start = (f32[3,4,4,128]{3,2,1,0:T(4,128)S(1)}, f32[3,4,4,128]{3,2,1,0:T(4,128)}, u32[]{:S(2)}) copy-start(f32[3,4,4,128]{3,2,1,0:T(4,128)} %param.23) | copy-start | bytes 73732
  1.4 45.4 %copy-start.12 = (f32[8]{0:T(128)S(1)}, f32[8]{0:T(128)}, u32[]{:S(2)}) copy-start(f32[8]{0:T(128)} %constant.93.clone) | copy-start | bytes 100
  2.8 44.1 %copy-start.15 = (f32[8]{0:T(128)S(1)}, f32[8]{0:T(128)}, u32[]{:S(2)}) copy-start(f32[8]{0:T(128)} %constant.94.clone) | copy-start | bytes 100
  2.8 44.1 %copy-start.14 = (f32[8]{0:T(128)S(1)}, f32[8]{0:T(128)}, u32[]{:S(2)}) copy-start(f32[8]{0:T(128)} %constant.95.clone) | copy-start | bytes 100
  2.8 44.2 %copy-start.13 = (f32[8]{0:T(128)S(1)}, f32[8]{0:T(128)}, u32[]{:S(2)}) copy-start(f32[8]{0:T(128)} %constant.96.clone) | copy-start | bytes 100
  2.8 44.4 %copy-start.11 = (f32[8]{0:T(128)S(1)}, f32[8]{0:T(128)}, u32[]{:S(2)}) copy-start(f32[8]{0:T(128)} %constant.98.clone) | copy-start | bytes 100
  2.8 44.4 %copy-start.10 = (f32[8]{0:T(128)S(1)}, f32[8]{0:T(128)}, u32[]{:S(2)}) copy-start(f32[8]{0:T(128)} %constant.99.clone) | copy-start | bytes 100
  2.8 44.5 %copy-start.9 = (f32[8]{0:T(128)S(1)}, f32[8]{0:T(128)}, u32[]{:S(2)}) copy-start(f32[8]{0:T(128)} %constant.100.clone) | copy-start | bytes 100
  2.8 44.6 %copy-start.8 = (f32[8]{0:T(128)S(1)}, f32[8]{0:T(128)}, u32[]{:S(2)}) copy-start(f32[8]{0:T(128)} %constant.101.clone) | copy-start | bytes 100
  7.6 23.4 %all-to-all-start = ((f32[4,128,16]{2,0,1:T(4,128)}), f32[4,128,16]{2,0,1:T(4,128)S(1)}, u32[]{:S(2)}, u32[]{:S(2)}) async-start(f32[4,128,16]{2,0,1:T(4,128)} %copy.54), calls=%async_computation | async-start | bytes 524288 | tf_op jit(solution)/shard_map/all_to_all | solution.py:215
  19.2 5.7 %collective-permute-start.8 = (f32[8,1,4,128]{3,2,1,0:T(4,128)S(1)}, f32[8,1,4,128]{3,2,1,0:T(4,128)S(1)}, u32[]{:S(2)}, u32[]{:S(2)}) collective-permute-start(f32[8,1,4,128]{3,2,1,0:T(4,128)S(1)} %get-tuple-element.60), channel_id=1, source_target_pairs={{8,0},{16,8},{24,16},{32,24},{40,32},{48,40},{56,48},{64,56},{72,6... | collective-permute-start | bytes 49160 | tf_op jit(solution)/shard_map/ppermute | solution.py:22
  22.2 3.4 %collective-permute-start.7 = (f32[8,1,4,128]{3,2,1,0:T(4,128)S(1)}, f32[8,1,4,128]{3,2,1,0:T(4,128)S(1)}, u32[]{:S(2)}, u32[]{:S(2)}) collective-permute-start(f32[8,1,4,128]{3,2,1,0:T(4,128)S(1)} %get-tuple-element.59), channel_id=1, source_target_pairs={{0,8},{8,16},{16,24},{24,32},{32,40},{40,48},{48,56},{56,64},{64,7... | collective-permute-start | bytes 49160 | tf_op jit(solution)/shard_map/ppermute | solution.py:21
  25.7 19.6 %collective-permute-start.10 = (f32[8,6,1,128]{3,2,1,0:T(1,128)S(1)}, f32[8,6,1,128]{3,2,1,0:T(1,128)S(1)}, u32[]{:S(2)}, u32[]{:S(2)}) collective-permute-start(f32[8,6,1,128]{3,2,1,0:T(1,128)S(1)} %get-tuple-element.57), channel_id=1, source_target_pairs={{1,0},{2,1},{3,2},{4,3},{5,4},{6,5},{7,6},{9,8},{10,9},{11,10},{12... | collective-permute-start | bytes 73736 | tf_op jit(solution)/shard_map/ppermute | solution.py:22
  27.0 19.6 %collective-permute-start.9 = (f32[8,6,1,128]{3,2,1,0:T(1,128)S(1)}, f32[8,6,1,128]{3,2,1,0:T(1,128)S(1)}, u32[]{:S(2)}, u32[]{:S(2)}) collective-permute-start(f32[8,6,1,128]{3,2,1,0:T(1,128)S(1)} %get-tuple-element.58), channel_id=1, source_target_pairs={{0,1},{1,2},{2,3},{3,4},{4,5},{5,6},{6,7},{8,9},{9,10},{10,11},{11... | collective-permute-start | bytes 73736 | tf_op jit(solution)/shard_map/ppermute | solution.py:21
  34.0 17.0 %collective-permute-start = (f32[4,1,16,1024]{3,2,1,0:T(8,128)S(1)}, f32[4,1,16,1024]{3,2,1,0:T(8,128)S(1)}, u32[]{:S(2)}, u32[]{:S(2)}) collective-permute-start(f32[4,1,16,1024]{3,2,1,0:T(8,128)S(1)} %get-tuple-element.46), channel_id=1, source_target_pairs={{0,8},{8,16},{16,24},{24,32},{32,40},{40,48},{48,56},{56,64},{64,7... | collective-permute-start | bytes 786440 | tf_op jit(solution)/shard_map/ppermute | solution.py:30
  38.8 12.2 %collective-permute-start.1 = (f32[4,1,16,1024]{3,2,1,0:T(8,128)S(1)}, f32[4,1,16,1024]{3,2,1,0:T(8,128)S(1)}, u32[]{:S(2)}, u32[]{:S(2)}) collective-permute-start(f32[4,1,16,1024]{3,2,1,0:T(8,128)S(1)} %get-tuple-element.45), channel_id=1, source_target_pairs={{8,0},{16,8},{24,16},{32,24},{40,32},{48,40},{56,48},{64,56},{72,6... | collective-permute-start | bytes 786440 | tf_op jit(solution)/shard_map/ppermute | solution.py:30
  40.7 7.4 %collective-permute-start.2 = (f32[4,8,1,1024]{3,2,1,0:T(1,128)S(1)}, f32[4,8,1,1024]{3,2,1,0:T(1,128)S(1)}, u32[]{:S(2)}, u32[]{:S(2)}) collective-permute-start(f32[4,8,1,1024]{3,2,1,0:T(1,128)S(1)} %get-tuple-element.44), channel_id=1, source_target_pairs={{0,1},{1,2},{2,3},{3,4},{4,5},{5,6},{6,7},{8,9},{9,10},{10,11},{11... | collective-permute-start | bytes 393224 | tf_op jit(solution)/shard_map/ppermute | solution.py:30
  45.3 5.7 %collective-permute-start.3 = (f32[4,8,1,1024]{3,2,1,0:T(1,128)S(1)}, f32[4,8,1,1024]{3,2,1,0:T(1,128)S(1)}, u32[]{:S(2)}, u32[]{:S(2)}) collective-permute-start(f32[4,8,1,1024]{3,2,1,0:T(1,128)S(1)} %get-tuple-element.43), channel_id=1, source_target_pairs={{1,0},{2,1},{3,2},{4,3},{5,4},{6,5},{7,6},{9,8},{10,9},{11,10},{12... | collective-permute-start | bytes 393224 | tf_op jit(solution)/shard_map/ppermute | solution.py:30
  48.1 2.9 %copy-start.5 = (f32[4,8,1,1024]{3,2,1,0:T(1,128)}, f32[4,8,1,1024]{3,2,1,0:T(1,128)S(1)}, u32[]{:S(2)}) copy-start(f32[4,8,1,1024]{3,2,1,0:T(1,128)S(1)} %collective-permute-done.2.y_lo_ref) | copy-start | bytes 393220
  51.0 0.6 copy-start.6
  51.0 0.8 copy-start.3
  51.8 0.7 copy-start.4
  59.2 33.5 %collective-permute-start.4 = (f32[4,16,1024]{2,1,0:T(8,128)}, f32[4,16,1024]{2,1,0:T(8,128)S(1)}, u32[]{:S(2)}, u32[]{:S(2)}) collective-permute-start(f32[4,16,1024]{2,1,0:T(8,128)} %get-tuple-element.13), channel_id=1, source_target_pairs={{8,0},{16,8},{24,16},{32,24},{40,32},{48,40},{56,48},{64,56},{72,6... | collective-permute-start | bytes 786440 | tf_op jit(solution)/shard_map/ppermute | solution.py:30
  81.9 9.4 %collective-permute-start.6 = (f32[4,1024]{1,0:T(4,128)}, f32[4,1024]{1,0:T(4,128)S(1)}, u32[]{:S(2)}, u32[]{:S(2)}) collective-permute-start(f32[4,1024]{1,0:T(4,128)} %get-tuple-element.15), channel_id=1, source_target_pairs={{9,0},{10,1},{11,2},{12,3},{13,4},{14,5},{15,6},{17,8},{18,9},{19,... | collective-permute-start | bytes 49160 | tf_op jit(solution)/shard_map/ppermute | solution.py:108
  83.2 9.5 %collective-permute-start.5 = (f32[4,8,1024]{2,1,0:T(8,128)}, f32[4,8,1024]{2,1,0:T(8,128)S(1)}, u32[]{:S(2)}, u32[]{:S(2)}) collective-permute-start(f32[4,8,1024]{2,1,0:T(8,128)} %get-tuple-element.14), channel_id=1, source_target_pairs={{1,0},{2,1},{3,2},{4,3},{5,4},{6,5},{7,6},{9,8},{10,9},{11,10},{12... | collective-permute-start | bytes 393224 | tf_op jit(solution)/shard_map/ppermute | solution.py:30
  107.5 30.0 %all-to-all-start.1 = ((f32[4,128,16]{2,0,1:T(4,128)}), f32[4,128,16]{2,0,1:T(4,128)S(1)}, u32[]{:S(2)}, u32[]{:S(2)}) async-start(f32[4,128,16]{2,0,1:T(4,128)} %copy.57), calls=%async_computation.1 | async-start | bytes 524288 | tf_op jit(solution)/shard_map/all_to_all | solution.py:231
where the time goes:
time: 141 us; the launch traced here: 140 us
  starting transfers between devices  58.6 us (42%)
  other arithmetic  26.5 us (19%)
  waiting for transfers between devices  21.5 us (15%)
  matrix products  15.3 us (11%)
  local copies, waits for them, and re-layouts  9.28 us (7%)
  Pallas kernels  6.67 us (5%)
  between operations  2.03 us (1%)
    reduce_sum x1, other arithmetic, pair_sums(): jnp.sum(weight * other_tiles[3 + channel][:, :, None], axis=1)  20.8 us
    all_to_all x1, starting transfers between devices, step_body(): lax.all_to_all(answer_requests(table, fv_next.shape, arrived), ('gx', 'gy...  19.5 us
    ppermute x6, starting transfers between devices, from_behind(): return lax.ppermute(array, axis, pairs)  15.5 us
    all_to_all x1, starting transfers between devices, step_body(): lax.all_to_all(outgoing, ('gx', 'gy'), split_axis=1, concat_axis=1, tiled...  11.5 us
    dot_general x1, matrix products, answer_requests(): lax.dot_general(table, z_weight, (((1,), (0,)), ((), ())), precision=lax....  10.7 us
    all_to_all x1, waiting for transfers between devices, step_body(): lax.all_to_all(answer_requests(table, fv_next.shape, arrived), ('gx', 'gy...  9.88 us
    pallas_call x1, Pallas kernels, flux_sweep(): pl.pallas_call(flux_kernel, out_shape=(jax.ShapeDtypeStruct(state.shape,...  6.67 us
    ppermute x2, starting transfers between devices, padded_2(): before = lax.ppermute(last, axis, up)  6.57 us
  transfers between devices with their start and end apart: 13, of which 5 were waited for; matrix products, arithmetic and copies ran while one was open for 19% of the time, Pallas kernels for 0%

commit v1 on v0

--- a/solution.py
+++ b/solution.py
@@ -256,7 +256,10 @@
         shift = jnp.array([step_x, step_y, 0, 0, 0, 0, 0, 0], jnp.float32)[:, None, None, None]
         neighbours.append(window + shift)
     other_tiles = jnp.stack(neighbours, axis=3).reshape(8, tiles_x * tiles_y, 9 * tile_slots)
-    total = pair_sums(own_tiles, other_tiles)
+    half = own_tiles.shape[1] // 2
+    first_total = pair_sums(own_tiles[:, :half], other_tiles[:, :half])
+    second_total = pair_sums(own_tiles[:, half:], other_tiles[:, half:])
+    total = jnp.concatenate([first_total, second_total], axis=1)
     sph_accel = (FORCE_SCALE * total * own_tiles[7][None]).reshape(3, tiles_x, tiles_y, tile_slots)
     return (fv_next, buffer_state, sph_accel)
 

time: 141 us -> 136 us (0.965)
  waiting for transfers between devices: 21.5 us -> 18.3 us
    ppermute x6, waiting for transfers between devices: 4.28 us -> 0.02 us  [from_behind(): return lax.ppermute(array, axis, pairs)]
    unnamed x32 -> x24, local copies, waits for them, and re-layouts: 1.53 us -> 0.07 us
    reduce_sum x1 -> x2, other arithmetic: 20.8 us -> 20.8 us  [pair_sums(): jnp.sum(push_term * separation, axis=1) + VISCOSITY * drag_term]
  transfers between devices with their start and end apart: 13 -> 13, of which waited for: 5 -> 3; matrix products, arithmetic and copies ran while one was open for 19% -> 20% of each run, Pallas kernels for 0% -> 0%
where the time goes in v1:
time: 136 us; the launch traced here: 135 us
  starting transfers between devices  58 us (43%)
  other arithmetic  26.5 us (19%)
  waiting for transfers between devices  18.3 us (13%)
  matrix products  15.2 us (11%)
  local copies, waits for them, and re-layouts  8.54 us (6%)
  Pallas kernels  6.66 us (5%)
  between operations  1.98 us (1%)
    reduce_sum x2, other arithmetic, pair_sums(): jnp.sum(push_term * separation, axis=1) + VISCOSITY * drag_term  20.8 us
    all_to_all x1, starting transfers between devices, step_body(): lax.all_to_all(answer_requests(table, fv_next.shape, arrived), ('gx', 'gy...  18.2 us
    ppermute x6, starting transfers between devices, from_behind(): return lax.ppermute(array, axis, pairs)  16 us
    all_to_all x1, starting transfers between devices, step_body(): lax.all_to_all(outgoing, ('gx', 'gy'), split_axis=1, concat_axis=1, tiled...  11.5 us
    dot_general x1, matrix products, answer_requests(): lax.dot_general(table, z_weight, (((1,), (0,)), ((), ())), precision=lax....  10.5 us
    all_to_all x1, waiting for transfers between devices, step_body(): lax.all_to_all(answer_requests(table, fv_next.shape, arrived), ('gx', 'gy...  9.88 us
    ppermute x1, waiting for transfers between devices, from_diagonal(): return lax.ppermute(array, ('gx', 'gy'), pairs)  7.62 us
    pallas_call x1, Pallas kernels, flux_sweep(): pl.pallas_call(flux_kernel, out_shape=(jax.ShapeDtypeStruct(state.shape,...  6.66 us
  transfers between devices with their start and end apart: 13, of which 3 were waited for; matrix products, arithmetic and copies ran while one was open for 20% of the time, Pallas kernels for 0%

profile of v1, /device:TPU:1, one launch (start us, length us, event | category | flops | bytes accessed | tf_op | source)
XLA Modules:
  0.0 135.2 jit_solution(15594113671505678137)
XLA Ops:
  1.4 1.4 %fusion.35 = f32[1024]{0:T(1024)S(1)} fusion(s32[1024]{0:T(1024)} %bitcast.185, pred[1024]{0:T(1024)(128)(4,1)S(1)} %iota_compare_fusion.20), kind=kOutput, calls=%fused_computation.61 | convolution fusion | flops 270269440 | bytes 9216 | tf_op jit(solution)/shard_map/dot_general | solution.py:205
  2.8 0.7 convert_element_type.55
  3.5 0.7 compare_select_fusion.4
  4.2 0.7 reduce-precision_convert_fusion.3
  5.0 1.6 %fusion.5 = f32[12,2048]{1,0:T(8,128)S(1)} fusion(s32[1024]{0:T(1024)S(1)} %bitcast.186, bf16[4,1024]{1,0:T(4,128)(2,1)S(1)} %get-tuple-element.104, bf16[4,1024]{1,0:T(4,128)(2,1)S(1)} %get-tuple-element.103, bf16[4,1024]{1,0:T(4,128)(2,1)S(1)} %get-tuple-element.102), kind=kOutput, calls=%fused_computation.8 | convolution fusion | flops 52502528 | bytes 126976 | tf_op jit(solution)/shard_map/dot_general | solution.py:213
  6.6 0.1 all_to_all.14
  6.7 0.9 copy.37
  7.6 11.5 %all-to-all-start = ((f32[4,128,16]{2,0,1:T(4,128)}), f32[4,128,16]{2,0,1:T(4,128)S(1)}, u32[]{:S(2)}, u32[]{:S(2)}) async-start(f32[4,128,16]{2,0,1:T(4,128)} %copy.37), calls=%async_computation | async-start | bytes 524288 | tf_op jit(solution)/shard_map/all_to_all | solution.py:215
  19.2 3.0 %collective-permute-start.8 = (f32[8,1,4,128]{3,2,1,0:T(4,128)S(1)}, f32[8,1,4,128]{3,2,1,0:T(4,128)S(1)}, u32[]{:S(2)}, u32[]{:S(2)}) collective-permute-start(f32[8,1,4,128]{3,2,1,0:T(4,128)S(1)} %get-tuple-element.72), channel_id=1, source_target_pairs={{8,0},{16,8},{24,16},{32,24},{40,32},{48,40},{56,48},{64,56},{72,6... | collective-permute-start | bytes 49160 | tf_op jit(solution)/shard_map/ppermute | solution.py:22
  22.2 2.6 %collective-permute-start.7 = (f32[8,1,4,128]{3,2,1,0:T(4,128)S(1)}, f32[8,1,4,128]{3,2,1,0:T(4,128)S(1)}, u32[]{:S(2)}, u32[]{:S(2)}) collective-permute-start(f32[8,1,4,128]{3,2,1,0:T(4,128)S(1)} %get-tuple-element.71), channel_id=1, source_target_pairs={{0,8},{8,16},{16,24},{24,32},{32,40},{40,48},{48,56},{56,64},{64,7... | collective-permute-start | bytes 49160 | tf_op jit(solution)/shard_map/ppermute | solution.py:21
  24.9 0.8 collective-permute-done.7
  25.7 1.3 collective-permute-start.10
  27.0 4.0 %collective-permute-start.9 = (f32[8,6,1,128]{3,2,1,0:T(1,128)S(1)}, f32[8,6,1,128]{3,2,1,0:T(1,128)S(1)}, u32[]{:S(2)}, u32[]{:S(2)}) collective-permute-start(f32[8,6,1,128]{3,2,1,0:T(1,128)S(1)} %get-tuple-element.70), channel_id=1, source_target_pairs={{0,1},{1,2},{2,3},{3,4},{4,5},{5,6},{6,7},{8,9},{9,10},{10,11},{11... | collective-permute-start | bytes 73736 | tf_op jit(solution)/shard_map/ppermute | solution.py:21
  31.0 0.2 all_to_all.16
  31.2 1.1 fusion.106
  32.2 2.5 %fusion.105 = (f32[4,8,1,1024]{3,2,1,0:T(1,128)}, f32[4,8,1,1024]{3,2,1,0:T(1,128)}) fusion(f32[4,8,16,1024]{3,2,1,0:T(8,128)} %state_ref), kind=kLoop, calls=%fused_computation.248 | loop fusion | bytes 524288 | tf_op jit(solution)/shard_map/slice | solution.py:220
  34.7 4.8 %collective-permute-start = (f32[4,1,16,1024]{3,2,1,0:T(8,128)S(1)}, f32[4,1,16,1024]{3,2,1,0:T(8,128)}, u32[]{:S(2)}, u32[]{:S(2)}) collective-permute-start(f32[4,1,16,1024]{3,2,1,0:T(8,128)S(1)} %get-tuple-element.50), channel_id=1, source_target_pairs={{0,8},{8,16},{16,24},{24,32},{32,40},{40,48},{48,56},{56,64},{64,7... | collective-permute-start | bytes 786440 | tf_op jit(solution)/shard_map/ppermute | solution.py:30
  39.5 1.9 %collective-permute-start.1 = (f32[4,1,16,1024]{3,2,1,0:T(8,128)S(1)}, f32[4,1,16,1024]{3,2,1,0:T(8,128)}, u32[]{:S(2)}, u32[]{:S(2)}) collective-permute-start(f32[4,1,16,1024]{3,2,1,0:T(8,128)S(1)} %get-tuple-element.49), channel_id=1, source_target_pairs={{8,0},{16,8},{24,16},{32,24},{40,32},{48,40},{56,48},{64,56},{72,6... | collective-permute-start | bytes 786440 | tf_op jit(solution)/shard_map/ppermute | solution.py:30
  41.4 4.8 %collective-permute-start.2 = (f32[4,8,1,1024]{3,2,1,0:T(1,128)}, f32[4,8,1,1024]{3,2,1,0:T(1,128)}, u32[]{:S(2)}, u32[]{:S(2)}) collective-permute-start(f32[4,8,1,1024]{3,2,1,0:T(1,128)} %get-tuple-element.48), channel_id=1, source_target_pairs={{0,1},{1,2},{2,3},{3,4},{4,5},{5,6},{6,7},{8,9},{9,10},{10,11},{11... | collective-permute-start | bytes 393224 | tf_op jit(solution)/shard_map/ppermute | solution.py:30
  46.2 0.1 fusion.107
  46.5 0.1 broadcast_multiply_fusion
  46.6 1.3 collective-permute-start.3
  48.1 0.1 fusion.63
  48.2 0.1 fusion.60
  48.3 0.1 fusion.58
  48.5 0.1 fusion.56
  48.7 0.1 fusion.52
  48.8 0.1 fusion.49
  48.9 0.4 copy.43
  49.2 0.1 reshape.387
  49.4 10.4 %fusion.20 = (f32[8,128]{1,0:T(8,128)S(1)}, f32[8,128]{1,0:T(8,128)S(1)}, f32[8,128]{1,0:T(8,128)S(1)}, f32[8,128]{1,0:T(8,128)S(1)}, f32[8,128]{1,0:T(8,128)S(1...) fusion(f32[8,1152]{1,0:T(8,128)S(1)} %get-tuple-element.58, f32[8,128]{1,0:T(8,128)S(1)} %get-tuple-element.99, ...), kind=kLoop, calls=%fused_computation.37 | loop fusion | flops 34202624 | bytes 339968 | tf_op jit(solution)/shard_map/reduce_sum | solution.py:164
  59.8 10.4 %fusion.11 = (f32[8,128]{1,0:T(8,128)S(1)}, f32[8,128]{1,0:T(8,128)S(1)}, f32[8,128]{1,0:T(8,128)S(1)}, f32[8,128]{1,0:T(8,128)S(1)}, f32[8,128]{1,0:T(8,128)S(1...) fusion(f32[8,1152]{1,0:T(8,128)S(1)} %get-tuple-element.65, f32[8,128]{1,0:T(8,128)S(1)} %get-tuple-element.101, ...), kind=kLoop, calls=%fused_computation.28 | loop fusion | flops 34202624 | bytes 339968 | tf_op jit(solution)/shard_map/reduce_sum | solution.py:164
  70.3 6.7 %shard_map.193 = (f32[4,8,16,1024]{3,2,1,0:T(8,128)}, f32[4,16,1024]{2,1,0:T(8,128)}, f32[4,8,1024]{2,1,0:T(8,128)}, f32[4,1024]{1,0:T(4,128)}, f32[640,1024]{1,0:T(8,128)}) custom-call(f32[4,8,16,1024]{3,2,1,0:T(8,128)} %state_ref, f32[4,1,16,1024]{3,2,1,0:T(8,128)} %collective-permute-done.x_lo_ref, f32[4,1,16,1024]{3,2,1,0:T(8,128)} %collective-permute-done.1.x_hi_ref, ...), custom_call_target="tpu_custom_call" | custom-call | tf_op jit(solution)/shard_map/pallas_call | solution.py:88
  77.0 1.3 collective-permute-start.5
  78.3 1.9 %collective-permute-start.4 = (f32[4,16,1024]{2,1,0:T(8,128)}, f32[4,16,1024]{2,1,0:T(8,128)S(1)}, u32[]{:S(2)}, u32[]{:S(2)}) collective-permute-start(f32[4,16,1024]{2,1,0:T(8,128)} %get-tuple-element.13), channel_id=1, source_target_pairs={{8,0},{16,8},{24,16},{32,24},{40,32},{48,40},{56,48},{64,56},{72,6... | collective-permute-start | bytes 786440 | tf_op jit(solution)/shard_map/ppermute | solution.py:30
  80.2 1.5 %collective-permute-start.6 = (f32[4,1024]{1,0:T(4,128)}, f32[4,1024]{1,0:T(4,128)S(1)}, u32[]{:S(2)}, u32[]{:S(2)}) collective-permute-start(f32[4,1024]{1,0:T(4,128)} %get-tuple-element.15), channel_id=1, source_target_pairs={{9,0},{10,1},{11,2},{12,3},{13,4},{14,5},{15,6},{17,8},{18,9},{19,... | collective-permute-start | bytes 49160 | tf_op jit(solution)/shard_map/ppermute | solution.py:108
  81.7 7.6 %collective-permute-done.6 = f32[4,1024]{1,0:T(4,128)S(1)} collective-permute-done((f32[4,1024]{1,0:T(4,128)}, f32[4,1024]{1,0:T(4,128)S(1)}, u32[]{:S(2)}, u32[]{:S(2)}) %collective-permute-start.6) | collective-permute-done | bytes 16416 | tf_op jit(solution)/shard_map/ppermute | solution.py:108
  89.5 1.8 %dynamic_update_slice.3 = f32[640,1024]{1,0:T(8,128)} dynamic-update-slice(f32[640,1024]{1,0:T(8,128)} %get-tuple-element.12, f32[100,1024]{1,0:T(8,128)S(1)} %reshape.386, s32[]{:T(128)} %constant.78.clone.1, s32[]{:T(128)} %constant.79.clone.1) | dynamic-update-slice | bytes 819204 | tf_op jit(solution)/shard_map/dynamic_update_slice | solution.py:228
  91.3 10.5 %fusion = f32[640,2048]{1,0:T(8,128)S(1)} fusion(f32[640,1024]{1,0:T(8,128)} %dynamic_update_slice.3, f32[2048]{0:T(1024)S(1)} %bitcast.182, s32[2048]{0:T(1024)S(1)} %bitcast.183, f32[2048]{0:T(1024)S(1)} %bitcast.181, s32[2048]{0:T(1024)S(1)} %bitcast.184), kind=kOutput, calls=%fused_computation | convolution fusion | flops 8063549440 | bytes 7897088 | tf_op jit(solution)/shard_map/dot_general | solution.py:123
  101.8 0.6 fusion.39
  102.5 0.2 fusion.45
  103.1 0.9 copy.40
  103.9 18.2 %all-to-all-start.1 = ((f32[4,128,16]{2,0,1:T(4,128)}), f32[4,128,16]{2,0,1:T(4,128)S(1)}, u32[]{:S(2)}, u32[]{:S(2)}) async-start(f32[4,128,16]{2,0,1:T(4,128)} %copy.40), calls=%async_computation.1 | async-start | bytes 524288 | tf_op jit(solution)/shard_map/all_to_all | solution.py:231
  122.2 0.6 broadcast_multiply_fusion.3
  122.8 9.9 %all-to-all-done.1 = f32[4,128,16]{2,0,1:T(4,128)S(1)} async-done(((f32[4,128,16]{2,0,1:T(4,128)}), f32[4,128,16]{2,0,1:T(4,128)S(1)}, u32[]{:S(2)}, u32[]{:S(2)}) %all-to-all-start.1) | async-done | bytes 32800 | tf_op jit(solution)/shard_map/all_to_all | solution.py:231
  132.7 0.2 all_to_all.18
  132.9 1.7 %fusion.4 = f32[12,1024]{1,0:T(8,128)S(1)} fusion(s32[1024]{0:T(1024)S(1)} %bitcast.187, bf16[4,2048]{1,0:T(4,128)(2,1)S(1)} %get-tuple-element.74, bf16[4,2048]{1,0:T(4,128)(2,1)S(1)} %get-tuple-element.75, bf16[4,2048]{1,0:T(4,128)(2,1)S(1)} %get-tuple-element.73), kind=kOutput, calls=%fused_computation.7 | convolution fusion | flops 52576256 | bytes 102400 | tf_op jit(solution)/shard_map/dot_general | solution.py:235
  134.5 0.6 fusion.78
  (71 shorter events, 1.3 us)
Async XLA Ops:
  0.6 18.5 %copy-start.3 = (s32[4,4]{1,0:T(4,128)S(1)}, s32[4,4]{1,0:T(4,128)}, u32[]{:S(2)}) copy-start(s32[4,4]{1,0:T(4,128)} %param.26) | copy-start | bytes 196
  0.6 18.5 %copy-start.1 = (f32[3,4,4,128]{3,2,1,0:T(4,128)S(1)}, f32[3,4,4,128]{3,2,1,0:T(4,128)}, u32[]{:S(2)}) copy-start(f32[3,4,4,128]{3,2,1,0:T(4,128)} %param.24) | copy-start | bytes 73732
  0.7 18.5 %copy-start.2 = (f32[4,4,128]{2,1,0:T(4,128)S(1)}, f32[4,4,128]{2,1,0:T(4,128)}, u32[]{:S(2)}) copy-start(f32[4,4,128]{2,1,0:T(4,128)} %param.25) | copy-start | bytes 24580
  0.7 18.5 %copy-start = (f32[3,4,4,128]{3,2,1,0:T(4,128)S(1)}, f32[3,4,4,128]{3,2,1,0:T(4,128)}, u32[]{:S(2)}) copy-start(f32[3,4,4,128]{3,2,1,0:T(4,128)} %param.23) | copy-start | bytes 73732
  2.8 45.3 %copy-start.8 = (f32[8]{0:T(128)S(1)}, f32[8]{0:T(128)}, u32[]{:S(2)}) copy-start(f32[8]{0:T(128)} %constant.93.clone) | copy-start | bytes 100
  2.8 45.4 %copy-start.11 = (f32[8]{0:T(128)S(1)}, f32[8]{0:T(128)}, u32[]{:S(2)}) copy-start(f32[8]{0:T(128)} %constant.94.clone) | copy-start | bytes 100
  2.8 45.4 %copy-start.10 = (f32[8]{0:T(128)S(1)}, f32[8]{0:T(128)}, u32[]{:S(2)}) copy-start(f32[8]{0:T(128)} %constant.95.clone) | copy-start | bytes 100
  4.9 43.4 %copy-start.9 = (f32[8]{0:T(128)S(1)}, f32[8]{0:T(128)}, u32[]{:S(2)}) copy-start(f32[8]{0:T(128)} %constant.96.clone) | copy-start | bytes 100
  4.9 43.5 %copy-start.7 = (f32[8]{0:T(128)S(1)}, f32[8]{0:T(128)}, u32[]{:S(2)}) copy-start(f32[8]{0:T(128)} %constant.98.clone) | copy-start | bytes 100
  5.0 43.6 %copy-start.6 = (f32[8]{0:T(128)S(1)}, f32[8]{0:T(128)}, u32[]{:S(2)}) copy-start(f32[8]{0:T(128)} %constant.99.clone) | copy-start | bytes 100
  5.0 43.7 %copy-start.5 = (f32[8]{0:T(128)S(1)}, f32[8]{0:T(128)}, u32[]{:S(2)}) copy-start(f32[8]{0:T(128)} %constant.100.clone) | copy-start | bytes 100
  5.0 43.8 %copy-start.4 = (f32[8]{0:T(128)S(1)}, f32[8]{0:T(128)}, u32[]{:S(2)}) copy-start(f32[8]{0:T(128)} %constant.101.clone) | copy-start | bytes 100
  7.6 23.4 %all-to-all-start = ((f32[4,128,16]{2,0,1:T(4,128)}), f32[4,128,16]{2,0,1:T(4,128)S(1)}, u32[]{:S(2)}, u32[]{:S(2)}) async-start(f32[4,128,16]{2,0,1:T(4,128)} %copy.37), calls=%async_computation | async-start | bytes 524288 | tf_op jit(solution)/shard_map/all_to_all | solution.py:215
  19.2 5.7 %collective-permute-start.8 = (f32[8,1,4,128]{3,2,1,0:T(4,128)S(1)}, f32[8,1,4,128]{3,2,1,0:T(4,128)S(1)}, u32[]{:S(2)}, u32[]{:S(2)}) collective-permute-start(f32[8,1,4,128]{3,2,1,0:T(4,128)S(1)} %get-tuple-element.72), channel_id=1, source_target_pairs={{8,0},{16,8},{24,16},{32,24},{40,32},{48,40},{56,48},{64,56},{72,6... | collective-permute-start | bytes 49160 | tf_op jit(solution)/shard_map/ppermute | solution.py:22
  22.2 3.4 %collective-permute-start.7 = (f32[8,1,4,128]{3,2,1,0:T(4,128)S(1)}, f32[8,1,4,128]{3,2,1,0:T(4,128)S(1)}, u32[]{:S(2)}, u32[]{:S(2)}) collective-permute-start(f32[8,1,4,128]{3,2,1,0:T(4,128)S(1)} %get-tuple-element.71), channel_id=1, source_target_pairs={{0,8},{8,16},{16,24},{24,32},{32,40},{40,48},{48,56},{56,64},{64,7... | collective-permute-start | bytes 49160 | tf_op jit(solution)/shard_map/ppermute | solution.py:21
  25.7 20.9 %collective-permute-start.10 = (f32[8,6,1,128]{3,2,1,0:T(1,128)S(1)}, f32[8,6,1,128]{3,2,1,0:T(1,128)S(1)}, u32[]{:S(2)}, u32[]{:S(2)}) collective-permute-start(f32[8,6,1,128]{3,2,1,0:T(1,128)S(1)} %get-tuple-element.69), channel_id=1, source_target_pairs={{1,0},{2,1},{3,2},{4,3},{5,4},{6,5},{7,6},{9,8},{10,9},{11,10},{12... | collective-permute-start | bytes 73736 | tf_op jit(solution)/shard_map/ppermute | solution.py:22
  27.0 21.0 %collective-permute-start.9 = (f32[8,6,1,128]{3,2,1,0:T(1,128)S(1)}, f32[8,6,1,128]{3,2,1,0:T(1,128)S(1)}, u32[]{:S(2)}, u32[]{:S(2)}) collective-permute-start(f32[8,6,1,128]{3,2,1,0:T(1,128)S(1)} %get-tuple-element.70), channel_id=1, source_target_pairs={{0,1},{1,2},{2,3},{3,4},{4,5},{5,6},{6,7},{8,9},{9,10},{10,11},{11... | collective-permute-start | bytes 73736 | tf_op jit(solution)/shard_map/ppermute | solution.py:21
  34.7 35.6 %collective-permute-start = (f32[4,1,16,1024]{3,2,1,0:T(8,128)S(1)}, f32[4,1,16,1024]{3,2,1,0:T(8,128)}, u32[]{:S(2)}, u32[]{:S(2)}) collective-permute-start(f32[4,1,16,1024]{3,2,1,0:T(8,128)S(1)} %get-tuple-element.50), channel_id=1, source_target_pairs={{0,8},{8,16},{16,24},{24,32},{32,40},{40,48},{48,56},{56,64},{64,7... | collective-permute-start | bytes 786440 | tf_op jit(solution)/shard_map/ppermute | solution.py:30
  39.5 30.8 %collective-permute-start.1 = (f32[4,1,16,1024]{3,2,1,0:T(8,128)S(1)}, f32[4,1,16,1024]{3,2,1,0:T(8,128)}, u32[]{:S(2)}, u32[]{:S(2)}) collective-permute-start(f32[4,1,16,1024]{3,2,1,0:T(8,128)S(1)} %get-tuple-element.49), channel_id=1, source_target_pairs={{8,0},{16,8},{24,16},{32,24},{40,32},{48,40},{56,48},{64,56},{72,6... | collective-permute-start | bytes 786440 | tf_op jit(solution)/shard_map/ppermute | solution.py:30
  41.4 28.9 %collective-permute-start.2 = (f32[4,8,1,1024]{3,2,1,0:T(1,128)}, f32[4,8,1,1024]{3,2,1,0:T(1,128)}, u32[]{:S(2)}, u32[]{:S(2)}) collective-permute-start(f32[4,8,1,1024]{3,2,1,0:T(1,128)} %get-tuple-element.48), channel_id=1, source_target_pairs={{0,1},{1,2},{2,3},{3,4},{4,5},{5,6},{6,7},{8,9},{9,10},{10,11},{11... | collective-permute-start | bytes 393224 | tf_op jit(solution)/shard_map/ppermute | solution.py:30
  46.6 23.7 %collective-permute-start.3 = (f32[4,8,1,1024]{3,2,1,0:T(1,128)}, f32[4,8,1,1024]{3,2,1,0:T(1,128)}, u32[]{:S(2)}, u32[]{:S(2)}) collective-permute-start(f32[4,8,1,1024]{3,2,1,0:T(1,128)} %get-tuple-element.47), channel_id=1, source_target_pairs={{1,0},{2,1},{3,2},{4,3},{5,4},{6,5},{7,6},{9,8},{10,9},{11,10},{12... | collective-permute-start | bytes 393224 | tf_op jit(solution)/shard_map/ppermute | solution.py:30
  77.0 12.4 %collective-permute-start.5 = (f32[4,8,1024]{2,1,0:T(8,128)}, f32[4,8,1024]{2,1,0:T(8,128)S(1)}, u32[]{:S(2)}, u32[]{:S(2)}) collective-permute-start(f32[4,8,1024]{2,1,0:T(8,128)} %get-tuple-element.14), channel_id=1, source_target_pairs={{1,0},{2,1},{3,2},{4,3},{5,4},{6,5},{7,6},{9,8},{10,9},{11,10},{12... | collective-permute-start | bytes 393224 | tf_op jit(solution)/shard_map/ppermute | solution.py:30
  78.3 11.1 %collective-permute-start.4 = (f32[4,16,1024]{2,1,0:T(8,128)}, f32[4,16,1024]{2,1,0:T(8,128)S(1)}, u32[]{:S(2)}, u32[]{:S(2)}) collective-permute-start(f32[4,16,1024]{2,1,0:T(8,128)} %get-tuple-element.13), channel_id=1, source_target_pairs={{8,0},{16,8},{24,16},{32,24},{40,32},{48,40},{56,48},{64,56},{72,6... | collective-permute-start | bytes 786440 | tf_op jit(solution)/shard_map/ppermute | solution.py:30
  80.2 9.1 %collective-permute-start.6 = (f32[4,1024]{1,0:T(4,128)}, f32[4,1024]{1,0:T(4,128)S(1)}, u32[]{:S(2)}, u32[]{:S(2)}) collective-permute-start(f32[4,1024]{1,0:T(4,128)} %get-tuple-element.15), channel_id=1, source_target_pairs={{9,0},{10,1},{11,2},{12,3},{13,4},{14,5},{15,6},{17,8},{18,9},{19,... | collective-permute-start | bytes 49160 | tf_op jit(solution)/shard_map/ppermute | solution.py:108
  103.9 28.7 %all-to-all-start.1 = ((f32[4,128,16]{2,0,1:T(4,128)}), f32[4,128,16]{2,0,1:T(4,128)S(1)}, u32[]{:S(2)}, u32[]{:S(2)}) async-start(f32[4,128,16]{2,0,1:T(4,128)} %copy.40), calls=%async_computation.1 | async-start | bytes 524288 | tf_op jit(solution)/shard_map/all_to_all | solution.py:231

commit v2 on v0

--- a/solution.py
+++ b/solution.py
@@ -9,19 +9,6 @@
 STEP_RATIO = 0.3
 VISCOSITY = 0.02
 FORCE_SCALE = 0.1
-
-
-def padded_2(array, sides, width):
-    for axis, dim in sides:
-        count, length = (lax.axis_size(axis), array.shape[dim])
-        up = [(i, (i + 1) % count) for i in range(count - 1)]
-        down = [(j, i) for i, j in up]
-        last = lax.slice_in_dim(array, length - width, length, axis=dim)
-        leading = lax.slice_in_dim(array, 0, width, axis=dim)
-        before = lax.ppermute(last, axis, up)
-        after = lax.ppermute(leading, axis, down)
-        array = jnp.concatenate([before, array, after], axis=dim)
-    return array
 
 
 def from_behind(array, axis, by):
@@ -97,6 +84,16 @@
     )(state, x_lo, x_hi, y_lo, y_hi)
 
 
+def packed_permute(arrays, axis, by):
+    flat = jnp.concatenate([array.reshape(-1) for array in arrays])
+    moved = from_behind(flat, axis, by)
+    parts, offset = [], 0
+    for array in arrays:
+        parts.append(moved[offset : offset + array.size].reshape(array.shape))
+        offset += array.size
+    return parts
+
+
 def from_diagonal(array):
     count_x = lax.axis_size("gx")
     count_y = lax.axis_size("gy")
@@ -190,6 +187,11 @@
 ):
     grid_x = lax.axis_size("gx")
     grid_y = lax.axis_size("gy")
+    tiles_x, tiles_y, tile_slots = sph_press.shape
+    tile_live = (
+        jnp.arange(tile_slots, dtype=jnp.int32)[None, None, :] < tile_count[:, :, None]
+    ).astype(jnp.float32)
+    packed = jnp.concatenate([sph_offset, sph_vel, sph_press[None], tile_live[None]], axis=0)
     devices = grid_x * grid_y
     buffer_rows = buffer_cell.shape[0]
     capacity = 2 * buffer_rows // devices
@@ -213,11 +215,13 @@
         jnp.dot(pieces(request), selector, preferred_element_type=jnp.float32), request.shape[0]
     )
     arrived = lax.all_to_all(outgoing, ("gx", "gy"), split_axis=1, concat_axis=1, tiled=True)
-    fv_state, arrived = lax.optimization_barrier((fv_state, arrived))
-    x_lo = from_behind(fv_state[:, -1:], "gx", 1)
-    x_hi = from_behind(fv_state[:, :1], "gx", -1)
-    y_lo = from_behind(fv_state[:, :, -1:], "gy", 1)
-    y_hi = from_behind(fv_state[:, :, :1], "gy", -1)
+    fv_state, packed, arrived = lax.optimization_barrier((fv_state, packed, arrived))
+    x_lo, sph_before = packed_permute([fv_state[:, -1:], packed[:, -1:]], "gx", 1)
+    x_hi, sph_after = packed_permute([fv_state[:, :1], packed[:, :1]], "gx", -1)
+    framed = jnp.concatenate([sph_before, packed, sph_after], axis=1)
+    y_lo, sph_left = packed_permute([fv_state[:, :, -1:], framed[:, :, -1:]], "gy", 1)
+    y_hi, sph_right = packed_permute([fv_state[:, :, :1], framed[:, :, :1]], "gy", -1)
+    framed = jnp.concatenate([sph_left, framed, sph_right], axis=2)
     fv_next, first_row, first_column, first_corner, table = flux_sweep(
         fv_state, x_lo, x_hi, y_lo, y_hi
     )
@@ -241,12 +245,6 @@
         returned.shape[0],
     )
     buffer_state = jnp.where(is_live[None, :], picked, 0.0)
-    tiles_x, tiles_y, tile_slots = sph_press.shape
-    tile_live = (
-        jnp.arange(tile_slots, dtype=jnp.int32)[None, None, :] < tile_count[:, :, None]
-    ).astype(jnp.float32)
-    packed = jnp.concatenate([sph_offset, sph_vel, sph_press[None], tile_live[None]], axis=0)
-    framed = padded_2(packed, (("gx", 1), ("gy", 2)), 1)
     own_tiles = packed.reshape(8, tiles_x * tiles_y, tile_slots)
     neighbours = []
     for corner in range(9):

time: 141 us -> 131 us (0.929)
  starting transfers between devices: 58.6 us -> 45.6 us
  waiting for transfers between devices: 21.5 us -> 23.4 us
  local copies, waits for them, and re-layouts: 9.28 us -> 10.8 us
    ppermute x4 -> x0, starting transfers between devices: 10.8 us -> none  [the longest x2 6.57 us: padded_2(): before = lax.ppermute(last, axis, up)]
    all_to_all x1, waiting for transfers between devices: 0.01 us -> 10.3 us  [step_body(): lax.all_to_all(outgoing, ('gx', 'gy'), split_axis=1, concat_axis=1, tiled...]
    ppermute x1, waiting for transfers between devices: 6.56 us -> 0.01 us  [from_diagonal(): return lax.ppermute(array, ('gx', 'gy'), pairs)]
    reshape x0 -> x2, local copies, waits for them, and re-layouts: none -> 1.51 us  [packed_permute(): parts.append(moved[offset:offset + array.size].reshape(array.shape))]
    slice x3 -> x11, local copies, waits for them, and re-layouts: 2.84 us -> 4.21 us  [the longest x1 1.76 us: step_body(): fv_state[:, :, :1]]
  transfers between devices with their start and end apart: 13 -> 9, of which waited for: 5 -> 4; matrix products, arithmetic and copies ran while one was open for 19% -> 20% of each run, Pallas kernels for 0% -> 0%
where the time goes in v2:
time: 131 us; the launch traced here: 130 us
  starting transfers between devices  45.6 us (35%)
  other arithmetic  26.5 us (20%)
  waiting for transfers between devices  23.4 us (18%)
  matrix products  15.2 us (12%)
  local copies, waits for them, and re-layouts  10.8 us (8%)
  Pallas kernels  6.65 us (5%)
  between operations  2.03 us (2%)
    reduce_sum x1, other arithmetic, pair_sums(): jnp.sum(weight * other_tiles[3 + channel][:, :, None], axis=1)  20.8 us
    all_to_all x1, starting transfers between devices, step_body(): lax.all_to_all(answer_requests(table, fv_next.shape, arrived), ('gx', 'gy...  18.2 us
    ppermute x6, starting transfers between devices, from_behind(): return lax.ppermute(array, axis, pairs)  14.4 us
    all_to_all x1, starting transfers between devices, step_body(): lax.all_to_all(outgoing, ('gx', 'gy'), split_axis=1, concat_axis=1, tiled...  11.5 us
    dot_general x1, matrix products, answer_requests(): lax.dot_general(table, z_weight, (((1,), (0,)), ((), ())), precision=lax....  10.5 us
    all_to_all x1, waiting for transfers between devices, step_body(): lax.all_to_all(outgoing, ('gx', 'gy'), split_axis=1, concat_axis=1, tiled...  10.3 us
    all_to_all x1, waiting for transfers between devices, step_body(): lax.all_to_all(answer_requests(table, fv_next.shape, arrived), ('gx', 'gy...  9.88 us
    pallas_call x1, Pallas kernels, flux_sweep(): pl.pallas_call(flux_kernel, out_shape=(jax.ShapeDtypeStruct(state.shape,...  6.65 us
  transfers between devices with their start and end apart: 9, of which 4 were waited for; matrix products, arithmetic and copies ran while one was open for 20% of the time, Pallas kernels for 0%

profile of v2, /device:TPU:1, one launch (start us, length us, event | category | flops | bytes accessed | tf_op | source)
XLA Modules:
  0.0 130.1 jit_solution(12653663215422664176)
XLA Ops:
  1.4 1.4 %fusion.25 = f32[1024]{0:T(1024)S(1)} fusion(s32[1024]{0:T(1024)} %bitcast.179, pred[1024]{0:T(1024)(128)(4,1)S(1)} %iota_compare_fusion.19), kind=kOutput, calls=%fused_computation.40 | convolution fusion | flops 270269440 | bytes 9216 | tf_op jit(solution)/shard_map/dot_general | solution.py:207
  2.8 0.7 convert_element_type.47
  3.5 0.7 compare_select_fusion.4
  4.2 0.7 reduce-precision_convert_fusion.3
  4.9 1.6 %fusion.14 = f32[12,2048]{1,0:T(8,128)S(1)} fusion(s32[1024]{0:T(1024)S(1)} %bitcast.180, bf16[4,1024]{1,0:T(4,128)(2,1)S(1)} %get-tuple-element.90, bf16[4,1024]{1,0:T(4,128)(2,1)S(1)} %get-tuple-element.89, bf16[4,1024]{1,0:T(4,128)(2,1)S(1)} %get-tuple-element.88), kind=kOutput, calls=%fused_computation.28 | convolution fusion | flops 52502528 | bytes 126976 | tf_op jit(solution)/shard_map/dot_general | solution.py:215
  6.5 0.1 all_to_all.14
  6.6 0.9 copy.48
  7.5 11.5 %all-to-all-start = ((f32[4,128,16]{2,0,1:T(4,128)}), f32[4,128,16]{2,0,1:T(4,128)S(1)}, u32[]{:S(2)}, u32[]{:S(2)}) async-start(f32[4,128,16]{2,0,1:T(4,128)} %copy.48), calls=%async_computation | async-start | bytes 524288 | tf_op jit(solution)/shard_map/all_to_all | solution.py:217
  19.2 10.3 %all-to-all-done = f32[4,128,16]{2,0,1:T(4,128)S(1)} async-done(((f32[4,128,16]{2,0,1:T(4,128)}), f32[4,128,16]{2,0,1:T(4,128)S(1)}, u32[]{:S(2)}, u32[]{:S(2)}) %all-to-all-start) | async-done | bytes 32800 | tf_op jit(solution)/shard_map/all_to_all | solution.py:217
  29.5 0.2 all_to_all.16
  29.7 1.1 fusion.76
  30.9 3.3 %collective-permute-start.1 = (f32[69632]{0:T(1024)S(1)}, f32[69632]{0:T(1024)S(1)}, u32[]{:S(2)}, u32[]{:S(2)}) collective-permute-start(f32[69632]{0:T(1024)S(1)} %pad_maximum_fusion.2), channel_id=1, source_target_pairs={{8,0},{16,8},{24,16},{32,24},{40,32},{48,40},{56,48},{64,56},{72,6... | collective-permute-start | bytes 835592 | tf_op jit(solution)/shard_map/ppermute | solution.py:17
  34.2 2.3 %collective-permute-start = (f32[69632]{0:T(1024)S(1)}, f32[69632]{0:T(1024)S(1)}, u32[]{:S(2)}, u32[]{:S(2)}) collective-permute-start(f32[69632]{0:T(1024)S(1)} %pad_maximum_fusion.1), channel_id=1, source_target_pairs={{0,8},{8,16},{16,24},{24,32},{32,40},{40,48},{48,56},{56,64},{64,7... | collective-permute-start | bytes 835592 | tf_op jit(solution)/shard_map/ppermute | solution.py:17
  36.6 0.1 fusion.80
  36.8 0.1 broadcast_multiply_fusion
  37.0 1.8 %fusion.75 = (f32[4,8,1,1024]{3,2,1,0:T(1,128)S(1)}, f32[4,8,1,1024]{3,2,1,0:T(1,128)S(1)}) fusion(f32[4,8,16,1024]{3,2,1,0:T(8,128)} %state_ref), kind=kLoop, calls=%fused_computation.179 | loop fusion | bytes 524288 | tf_op jit(solution)/shard_map/slice | solution.py:223
  38.8 1.3 collective-permute-done
  40.1 1.3 collective-permute-start.3
  41.4 4.0 %collective-permute-start.2 = (f32[38912]{0:T(1024)S(1)}, f32[38912]{0:T(1024)S(1)}, u32[]{:S(2)}, u32[]{:S(2)}) collective-permute-start(f32[38912]{0:T(1024)S(1)} %pad_maximum_fusion.6), channel_id=1, source_target_pairs={{0,1},{1,2},{2,3},{3,4},{4,5},{5,6},{6,7},{8,9},{9,10},{10,11},{11... | collective-permute-start | bytes 466952 | tf_op jit(solution)/shard_map/ppermute | solution.py:17
  45.5 0.8 reshape.434.x_hi_ref
  46.3 0.7 reshape.431.x_lo_ref
  47.0 1.8 %collective-permute-done.3 = f32[38912]{0:T(1024)S(1)} collective-permute-done((f32[38912]{0:T(1024)S(1)}, f32[38912]{0:T(1024)S(1)}, u32[]{:S(2)}, u32[]{:S(2)}) %collective-permute-start.3) | collective-permute-done | bytes 155680 | tf_op jit(solution)/shard_map/ppermute | solution.py:17
  48.9 0.1 fusion.55
  49.0 0.1 fusion.53
  49.1 0.1 fusion.50
  49.2 0.1 fusion.48
  49.4 0.1 fusion.46
  49.5 0.1 fusion.44
  49.6 0.1 fusion.42
  49.7 0.1 fusion.39
  50.1 0.7 slice.286
  50.8 0.7 slice.285
  51.4 6.7 %shard_map.193 = (f32[4,8,16,1024]{3,2,1,0:T(8,128)}, f32[4,16,1024]{2,1,0:T(8,128)}, f32[4,8,1024]{2,1,0:T(8,128)}, f32[4,1024]{1,0:T(4,128)}, f32[640,1024]{1,0:T(8,128)}) custom-call(f32[4,8,16,1024]{3,2,1,0:T(8,128)} %state_ref, f32[4,1,16,1024]{3,2,1,0:T(8,128)} %reshape.431.x_lo_ref, f32[4,1,16,1024]{3,2,1,0:T(8,128)} %reshape.434.x_hi_ref, ...), custom_call_target="tpu_custom_call" | custom-call | tf_op jit(solution)/shard_map/pallas_call | solution.py:75
  58.1 2.3 %collective-permute-start.4 = (f32[4,16,1024]{2,1,0:T(8,128)}, f32[4,16,1024]{2,1,0:T(8,128)S(1)}, u32[]{:S(2)}, u32[]{:S(2)}) collective-permute-start(f32[4,16,1024]{2,1,0:T(8,128)} %get-tuple-element.15), channel_id=1, source_target_pairs={{8,0},{16,8},{24,16},{32,24},{40,32},{48,40},{56,48},{64,56},{72,6... | collective-permute-start | bytes 786440 | tf_op jit(solution)/shard_map/ppermute | solution.py:17
  60.4 1.3 collective-permute-start.5
  61.7 1.5 %collective-permute-start.6 = (f32[4,1024]{1,0:T(4,128)}, f32[4,1024]{1,0:T(4,128)S(1)}, u32[]{:S(2)}, u32[]{:S(2)}) collective-permute-start(f32[4,1024]{1,0:T(4,128)} %get-tuple-element.17), channel_id=1, source_target_pairs={{9,0},{10,1},{11,2},{12,3},{13,4},{14,5},{15,6},{17,8},{18,9},{19,... | collective-permute-start | bytes 49160 | tf_op jit(solution)/shard_map/ppermute | solution.py:105
  63.4 20.8 %multiply_reduce_fusion.2 = (f32[16,128]{1,0:T(8,128)S(1)}, f32[16,128]{1,0:T(8,128)S(1)}, f32[16,128]{1,0:T(8,128)S(1)}, f32[16,128]{1,0:T(8,128)S(1)}, f32[16,...) fusion(f32[16,1152]{1,0:T(8,128)S(1)} %get-tuple-element.95, f32[16,1152]{1,0:T(8,128)S(1)} %get-tuple-element.96, ...), kind=kLoop, calls=%fused_computation.18 | loop fusion | flops 68405248 | bytes 679936 | tf_op jit(solution)/shard_map/reduce_sum | solution.py:158
  84.4 1.8 %dynamic_update_slice.3 = f32[640,1024]{1,0:T(8,128)} dynamic-update-slice(f32[640,1024]{1,0:T(8,128)} %get-tuple-element.14, f32[100,1024]{1,0:T(8,128)S(1)} %reshape.441, s32[]{:T(128)} %constant.77.clone.1, s32[]{:T(128)} %constant.78.clone.1) | dynamic-update-slice | bytes 819204 | tf_op jit(solution)/shard_map/dynamic_update_slice | solution.py:232
  86.2 10.5 %fusion.9 = f32[640,2048]{1,0:T(8,128)S(1)} fusion(f32[640,1024]{1,0:T(8,128)} %dynamic_update_slice.3, f32[2048]{0:T(1024)S(1)} %bitcast.164, s32[2048]{0:T(1024)S(1)} %bitcast.166, f32[2048]{0:T(1024)S(1)} %bitcast.163, s32[2048]{0:T(1024)S(1)} %bitcast.167), kind=kOutput, calls=%fused_computation.20 | convolution fusion | flops 8063549440 | bytes 7897088 | tf_op jit(solution)/shard_map/dot_general | solution.py:120
  96.8 0.6 fusion.29
  97.4 0.2 fusion.35
  98.0 0.9 copy.51
  98.9 18.2 %all-to-all-start.1 = ((f32[4,128,16]{2,0,1:T(4,128)}), f32[4,128,16]{2,0,1:T(4,128)S(1)}, u32[]{:S(2)}, u32[]{:S(2)}) async-start(f32[4,128,16]{2,0,1:T(4,128)} %copy.51), calls=%async_computation.1 | async-start | bytes 524288 | tf_op jit(solution)/shard_map/all_to_all | solution.py:235
  117.1 0.6 maximum_multiply_fusion
  117.7 9.9 %all-to-all-done.1 = f32[4,128,16]{2,0,1:T(4,128)S(1)} async-done(((f32[4,128,16]{2,0,1:T(4,128)}), f32[4,128,16]{2,0,1:T(4,128)S(1)}, u32[]{:S(2)}, u32[]{:S(2)}) %all-to-all-start.1) | async-done | bytes 32800 | tf_op jit(solution)/shard_map/all_to_all | solution.py:235
  127.6 0.2 all_to_all.18
  127.8 1.7 %fusion.13 = f32[12,1024]{1,0:T(8,128)S(1)} fusion(s32[1024]{0:T(1024)S(1)} %bitcast.181, bf16[4,2048]{1,0:T(4,128)(2,1)S(1)} %get-tuple-element.72, bf16[4,2048]{1,0:T(4,128)(2,1)S(1)} %get-tuple-element.73, bf16[4,2048]{1,0:T(4,128)(2,1)S(1)} %get-tuple-element.71), kind=kOutput, calls=%fused_computation.27 | convolution fusion | flops 52576256 | bytes 102400 | tf_op jit(solution)/shard_map/dot_general | solution.py:239
  129.5 0.6 fusion.68
  (86 shorter events, 1.7 us)
Async XLA Ops:
  0.6 18.4 %copy-start.3 = (s32[4,4]{1,0:T(4,128)S(1)}, s32[4,4]{1,0:T(4,128)}, u32[]{:S(2)}) copy-start(s32[4,4]{1,0:T(4,128)} %param.26) | copy-start | bytes 196
  0.6 18.4 %copy-start.2 = (f32[4,4,128]{2,1,0:T(4,128)S(1)}, f32[4,4,128]{2,1,0:T(4,128)}, u32[]{:S(2)}) copy-start(f32[4,4,128]{2,1,0:T(4,128)} %param.25) | copy-start | bytes 24580
  0.7 18.4 %copy-start.1 = (f32[3,4,4,128]{3,2,1,0:T(4,128)S(1)}, f32[3,4,4,128]{3,2,1,0:T(4,128)}, u32[]{:S(2)}) copy-start(f32[3,4,4,128]{3,2,1,0:T(4,128)} %param.23) | copy-start | bytes 73732
  0.7 18.4 %copy-start = (f32[3,4,4,128]{3,2,1,0:T(4,128)S(1)}, f32[3,4,4,128]{3,2,1,0:T(4,128)}, u32[]{:S(2)}) copy-start(f32[3,4,4,128]{3,2,1,0:T(4,128)} %param.24) | copy-start | bytes 73732
  7.5 22.0 %all-to-all-start = ((f32[4,128,16]{2,0,1:T(4,128)}), f32[4,128,16]{2,0,1:T(4,128)S(1)}, u32[]{:S(2)}, u32[]{:S(2)}) async-start(f32[4,128,16]{2,0,1:T(4,128)} %copy.48), calls=%async_computation | async-start | bytes 524288 | tf_op jit(solution)/shard_map/all_to_all | solution.py:217
  19.0 29.9 %copy-start.8 = (f32[8]{0:T(128)S(1)}, f32[8]{0:T(128)}, u32[]{:S(2)}) copy-start(f32[8]{0:T(128)} %constant.92.clone) | copy-start | bytes 100
  19.1 29.9 %copy-start.11 = (f32[8]{0:T(128)S(1)}, f32[8]{0:T(128)}, u32[]{:S(2)}) copy-start(f32[8]{0:T(128)} %constant.93.clone) | copy-start | bytes 100
  19.1 30.0 %copy-start.10 = (f32[8]{0:T(128)S(1)}, f32[8]{0:T(128)}, u32[]{:S(2)}) copy-start(f32[8]{0:T(128)} %constant.94.clone) | copy-start | bytes 100
  19.1 30.1 %copy-start.9 = (f32[8]{0:T(128)S(1)}, f32[8]{0:T(128)}, u32[]{:S(2)}) copy-start(f32[8]{0:T(128)} %constant.95.clone) | copy-start | bytes 100
  29.5 19.8 %copy-start.7 = (f32[8]{0:T(128)S(1)}, f32[8]{0:T(128)}, u32[]{:S(2)}) copy-start(f32[8]{0:T(128)} %constant.97.clone) | copy-start | bytes 100
  29.5 19.9 %copy-start.6 = (f32[8]{0:T(128)S(1)}, f32[8]{0:T(128)}, u32[]{:S(2)}) copy-start(f32[8]{0:T(128)} %constant.98.clone) | copy-start | bytes 100
  29.7 19.9 %copy-start.5 = (f32[8]{0:T(128)S(1)}, f32[8]{0:T(128)}, u32[]{:S(2)}) copy-start(f32[8]{0:T(128)} %constant.99.clone) | copy-start | bytes 100
  29.7 19.9 %copy-start.4 = (f32[8]{0:T(128)S(1)}, f32[8]{0:T(128)}, u32[]{:S(2)}) copy-start(f32[8]{0:T(128)} %constant.100.clone) | copy-start | bytes 100
  30.9 7.9 %collective-permute-start.1 = (f32[69632]{0:T(1024)S(1)}, f32[69632]{0:T(1024)S(1)}, u32[]{:S(2)}, u32[]{:S(2)}) collective-permute-start(f32[69632]{0:T(1024)S(1)} %pad_maximum_fusion.2), channel_id=1, source_target_pairs={{8,0},{16,8},{24,16},{32,24},{40,32},{48,40},{56,48},{64,56},{72,6... | collective-permute-start | bytes 835592 | tf_op jit(solution)/shard_map/ppermute | solution.py:17
  34.2 5.8 %collective-permute-start = (f32[69632]{0:T(1024)S(1)}, f32[69632]{0:T(1024)S(1)}, u32[]{:S(2)}, u32[]{:S(2)}) collective-permute-start(f32[69632]{0:T(1024)S(1)} %pad_maximum_fusion.1), channel_id=1, source_target_pairs={{0,8},{8,16},{16,24},{24,32},{32,40},{40,48},{48,56},{56,64},{64,7... | collective-permute-start | bytes 835592 | tf_op jit(solution)/shard_map/ppermute | solution.py:17
  40.1 8.7 %collective-permute-start.3 = (f32[38912]{0:T(1024)S(1)}, f32[38912]{0:T(1024)S(1)}, u32[]{:S(2)}, u32[]{:S(2)}) collective-permute-start(f32[38912]{0:T(1024)S(1)} %pad_maximum_fusion.7), channel_id=1, source_target_pairs={{1,0},{2,1},{3,2},{4,3},{5,4},{6,5},{7,6},{9,8},{10,9},{11,10},{12... | collective-permute-start | bytes 466952 | tf_op jit(solution)/shard_map/ppermute | solution.py:17
  41.4 7.4 %collective-permute-start.2 = (f32[38912]{0:T(1024)S(1)}, f32[38912]{0:T(1024)S(1)}, u32[]{:S(2)}, u32[]{:S(2)}) collective-permute-start(f32[38912]{0:T(1024)S(1)} %pad_maximum_fusion.6), channel_id=1, source_target_pairs={{0,1},{1,2},{2,3},{3,4},{4,5},{5,6},{6,7},{8,9},{9,10},{10,11},{11... | collective-permute-start | bytes 466952 | tf_op jit(solution)/shard_map/ppermute | solution.py:17
  58.1 26.2 %collective-permute-start.4 = (f32[4,16,1024]{2,1,0:T(8,128)}, f32[4,16,1024]{2,1,0:T(8,128)S(1)}, u32[]{:S(2)}, u32[]{:S(2)}) collective-permute-start(f32[4,16,1024]{2,1,0:T(8,128)} %get-tuple-element.15), channel_id=1, source_target_pairs={{8,0},{16,8},{24,16},{32,24},{40,32},{48,40},{56,48},{64,56},{72,6... | collective-permute-start | bytes 786440 | tf_op jit(solution)/shard_map/ppermute | solution.py:17
  60.4 23.9 %collective-permute-start.5 = (f32[4,8,1024]{2,1,0:T(8,128)}, f32[4,8,1024]{2,1,0:T(8,128)S(1)}, u32[]{:S(2)}, u32[]{:S(2)}) collective-permute-start(f32[4,8,1024]{2,1,0:T(8,128)} %get-tuple-element.16), channel_id=1, source_target_pairs={{1,0},{2,1},{3,2},{4,3},{5,4},{6,5},{7,6},{9,8},{10,9},{11,10},{12... | collective-permute-start | bytes 393224 | tf_op jit(solution)/shard_map/ppermute | solution.py:17
  61.7 22.6 %collective-permute-start.6 = (f32[4,1024]{1,0:T(4,128)}, f32[4,1024]{1,0:T(4,128)S(1)}, u32[]{:S(2)}, u32[]{:S(2)}) collective-permute-start(f32[4,1024]{1,0:T(4,128)} %get-tuple-element.17), channel_id=1, source_target_pairs={{9,0},{10,1},{11,2},{12,3},{13,4},{14,5},{15,6},{17,8},{18,9},{19,... | collective-permute-start | bytes 49160 | tf_op jit(solution)/shard_map/ppermute | solution.py:105
  98.9 28.7 %all-to-all-start.1 = ((f32[4,128,16]{2,0,1:T(4,128)}), f32[4,128,16]{2,0,1:T(4,128)S(1)}, u32[]{:S(2)}, u32[]{:S(2)}) async-start(f32[4,128,16]{2,0,1:T(4,128)} %copy.51), calls=%async_computation.1 | async-start | bytes 524288 | tf_op jit(solution)/shard_map/all_to_all | solution.py:235

commit v3 on v2

--- a/solution.py
+++ b/solution.py
@@ -84,6 +84,13 @@
     )(state, x_lo, x_hi, y_lo, y_hi)
 
 
+def exchange(values, devices):
+    channels, slots = values.shape
+    rows = values.reshape(channels, devices, slots // devices).transpose(1, 0, 2)
+    moved = lax.all_to_all(rows.reshape(devices, -1), ("gx", "gy"), 0, 0, tiled=True)
+    return moved.reshape(devices, channels, slots // devices).transpose(1, 0, 2).reshape(channels, slots)
+
+
 def packed_permute(arrays, axis, by):
     flat = jnp.concatenate([array.reshape(-1) for array in arrays])
     moved = from_behind(flat, axis, by)
@@ -192,6 +199,12 @@
         jnp.arange(tile_slots, dtype=jnp.int32)[None, None, :] < tile_count[:, :, None]
     ).astype(jnp.float32)
     packed = jnp.concatenate([sph_offset, sph_vel, sph_press[None], tile_live[None]], axis=0)
+    x_lo, sph_before = packed_permute([fv_state[:, -1:], packed[:, -1:]], "gx", 1)
+    x_hi, sph_after = packed_permute([fv_state[:, :1], packed[:, :1]], "gx", -1)
+    framed = jnp.concatenate([sph_before, packed, sph_after], axis=1)
+    y_lo, sph_left = packed_permute([fv_state[:, :, -1:], framed[:, :, -1:]], "gy", 1)
+    y_hi, sph_right = packed_permute([fv_state[:, :, :1], framed[:, :, :1]], "gy", -1)
+    framed = jnp.concatenate([sph_left, framed, sph_right], axis=2)
     devices = grid_x * grid_y
     buffer_rows = buffer_cell.shape[0]
     capacity = 2 * buffer_rows // devices
@@ -214,14 +227,7 @@
     outgoing = joined(
         jnp.dot(pieces(request), selector, preferred_element_type=jnp.float32), request.shape[0]
     )
-    arrived = lax.all_to_all(outgoing, ("gx", "gy"), split_axis=1, concat_axis=1, tiled=True)
-    fv_state, packed, arrived = lax.optimization_barrier((fv_state, packed, arrived))
-    x_lo, sph_before = packed_permute([fv_state[:, -1:], packed[:, -1:]], "gx", 1)
-    x_hi, sph_after = packed_permute([fv_state[:, :1], packed[:, :1]], "gx", -1)
-    framed = jnp.concatenate([sph_before, packed, sph_after], axis=1)
-    y_lo, sph_left = packed_permute([fv_state[:, :, -1:], framed[:, :, -1:]], "gy", 1)
-    y_hi, sph_right = packed_permute([fv_state[:, :, :1], framed[:, :, :1]], "gy", -1)
-    framed = jnp.concatenate([sph_left, framed, sph_right], axis=2)
+    arrived = exchange(outgoing, devices)
     fv_next, first_row, first_column, first_corner, table = flux_sweep(
         fv_state, x_lo, x_hi, y_lo, y_hi
     )
@@ -232,9 +238,7 @@
     table = lax.dynamic_update_slice(
         table, extra.reshape(-1, extra.shape[-1]), (fv_next.size // fv_next.shape[-1], 0)
     )
-    returned = lax.all_to_all(
-        answer_requests(table, fv_next.shape, arrived), ("gx", "gy"), split_axis=1, concat_axis=1, tiled=True
-    )
+    returned = exchange(answer_requests(table, fv_next.shape, arrived), devices)
     picked = joined(
         lax.dot_general(
             pieces(returned),

time: 131 us -> 121 us (0.924)
  starting transfers between devices: 45.6 us -> 36.9 us
  waiting for transfers between devices: 23.4 us -> 21.4 us
    all_to_all x2, starting transfers between devices: 29.7 us -> 20.6 us  [exchange(): lax.all_to_all(rows.reshape(devices, -1), ('gx', 'gy'), 0, 0, tiled=True)]
    all_to_all x2, waiting for transfers between devices: 20.2 us -> 16.4 us  [exchange(): lax.all_to_all(rows.reshape(devices, -1), ('gx', 'gy'), 0, 0, tiled=True)]
    ppermute x6, waiting for transfers between devices: 3.15 us -> 5.06 us  [from_behind(): return lax.ppermute(array, axis, pairs)]
    concatenate x1 -> x2, other arithmetic: 0.02 us -> 1.56 us  [step_body(): jnp.concatenate([sph_offset, sph_vel, sph_press[None], tile_live[None]],...]
  transfers between devices with their start and end apart: 9 -> 9, of which waited for: 4 -> 3; matrix products, arithmetic and copies ran while one was open for 20% -> 25% of each run, Pallas kernels for 0% -> 0%
where the time goes in v3:
time: 121 us; the launch traced here: 120 us
  starting transfers between devices  36.9 us (30%)
  other arithmetic  25.9 us (21%)
  waiting for transfers between devices  21.4 us (18%)
  matrix products  15.2 us (13%)
  local copies, waits for them, and re-layouts  12 us (10%)
  Pallas kernels  6.66 us (6%)
  between operations  2.13 us (2%)
    reduce_sum x1, other arithmetic, pair_sums(): jnp.sum(weight * other_tiles[3 + channel][:, :, None], axis=1)  20.8 us
    all_to_all x2, starting transfers between devices, exchange(): lax.all_to_all(rows.reshape(devices, -1), ('gx', 'gy'), 0, 0, tiled=True)  20.6 us
    all_to_all x2, waiting for transfers between devices, exchange(): lax.all_to_all(rows.reshape(devices, -1), ('gx', 'gy'), 0, 0, tiled=True)  16.4 us
    ppermute x6, starting transfers between devices, from_behind(): return lax.ppermute(array, axis, pairs)  14.9 us
    dot_general x1, matrix products, answer_requests(): lax.dot_general(table, z_weight, (((1,), (0,)), ((), ())), precision=lax....  10.5 us
    pallas_call x1, Pallas kernels, flux_sweep(): pl.pallas_call(flux_kernel, out_shape=(jax.ShapeDtypeStruct(state.shape,...  6.66 us
    ppermute x6, waiting for transfers between devices, from_behind(): return lax.ppermute(array, axis, pairs)  5.06 us
  transfers between devices with their start and end apart: 9, of which 3 were waited for; matrix products, arithmetic and copies ran while one was open for 25% of the time, Pallas kernels for 0%

profile of v3, /device:TPU:1, one launch (start us, length us, event | category | flops | bytes accessed | tf_op | source)
XLA Modules:
  0.0 120.3 jit_solution(17713892613689645869)
XLA Ops:
  0.7 0.8 fusion.78
  1.5 1.1 fusion.83
  2.6 0.8 pad_maximum_fusion.22
  3.4 4.5 %collective-permute-start = (f32[69632]{0:T(1024)S(1)}, f32[69632]{0:T(1024)S(1)}, u32[]{:S(2)}, u32[]{:S(2)}) collective-permute-start(f32[69632]{0:T(1024)S(1)} %pad_maximum_fusion.1), channel_id=1, source_target_pairs={{0,8},{8,16},{16,24},{24,32},{32,40},{40,48},{48,56},{56,64},{64,7... | collective-permute-start | bytes 835592 | tf_op jit(solution)/shard_map/ppermute | solution.py:17
  8.0 1.9 %collective-permute-start.1 = (f32[69632]{0:T(1024)S(1)}, f32[69632]{0:T(1024)S(1)}, u32[]{:S(2)}, u32[]{:S(2)}) collective-permute-start(f32[69632]{0:T(1024)S(1)} %pad_maximum_fusion.2), channel_id=1, source_target_pairs={{8,0},{16,8},{24,16},{32,24},{40,32},{48,40},{56,48},{64,56},{72,6... | collective-permute-start | bytes 835592 | tf_op jit(solution)/shard_map/ppermute | solution.py:17
  10.6 1.4 %fusion.25 = f32[1024]{0:T(1024)S(1)} fusion(s32[1024]{0:T(1024)} %bitcast.181, pred[1024]{0:T(1024)(128)(4,1)S(1)} %iota_compare_fusion.20), kind=kOutput, calls=%fused_computation.40 | convolution fusion | flops 270269440 | bytes 9216 | tf_op jit(solution)/shard_map/dot_general | solution.py:220
  12.2 1.6 %fusion.14 = f32[12,2048]{1,0:T(8,128)S(1)} fusion(s32[1024]{0:T(1024)S(1)} %bitcast.182, bf16[4,1024]{1,0:T(4,128)(2,1)S(1)} %get-tuple-element.70, bf16[4,1024]{1,0:T(4,128)(2,1)S(1)} %get-tuple-element.69, bf16[4,1024]{1,0:T(4,128)(2,1)S(1)} %get-tuple-element.68), kind=kOutput, calls=%fused_computation.27 | convolution fusion | flops 52502528 | bytes 126976 | tf_op jit(solution)/shard_map/dot_general | solution.py:228
  13.8 0.1 reshape.729
  13.9 0.1 copy.74
  14.0 0.7 copy.75
  14.8 11.8 %all-to-all-start = ((f32[128,1,64]{2,1,0:T(1,128)}), f32[128,1,64]{2,1,0:T(1,128)S(1)}, u32[]{:S(2)}, u32[]{:S(2)}) async-start(f32[128,1,64]{2,1,0:T(1,128)} %copy.75), calls=%async_computation | async-start | bytes 131072 | tf_op jit(solution)/shard_map/all_to_all | solution.py:90
  26.6 1.8 %fusion.82 = (f32[4,8,1,1024]{3,2,1,0:T(1,128)S(1)}, f32[4,8,1,1024]{3,2,1,0:T(1,128)S(1)}) fusion(f32[4,8,16,1024]{3,2,1,0:T(8,128)} %state_ref.1), kind=kLoop, calls=%fused_computation.210 | loop fusion | bytes 524288 | tf_op jit(solution)/shard_map/slice | solution.py:206
  28.4 7.5 %all-to-all-done = f32[128,1,64]{2,1,0:T(1,128)S(1)} async-done(((f32[128,1,64]{2,1,0:T(1,128)}), f32[128,1,64]{2,1,0:T(1,128)S(1)}, u32[]{:S(2)}, u32[]{:S(2)}) %all-to-all-start) | async-done | bytes 32800 | tf_op jit(solution)/shard_map/all_to_all | solution.py:90
  36.1 0.1 copy.77
  36.2 0.1 convert_element_type.89
  36.3 0.1 copy.79
  36.6 0.1 copy.80
  36.8 0.1 squeeze.22
  36.9 0.1 copy.78
  37.2 0.1 broadcast_multiply_fusion
  37.3 0.1 fusion.71
  37.6 2.3 %collective-permute-start.2 = (f32[38912]{0:T(1024)S(1)}, f32[38912]{0:T(1024)S(1)}, u32[]{:S(2)}, u32[]{:S(2)}) collective-permute-start(f32[38912]{0:T(1024)S(1)} %pad_maximum_fusion.5), channel_id=1, source_target_pairs={{0,1},{1,2},{2,3},{3,4},{4,5},{5,6},{6,7},{8,9},{9,10},{10,11},{11... | collective-permute-start | bytes 466952 | tf_op jit(solution)/shard_map/ppermute | solution.py:17
  39.9 1.3 %collective-permute-start.3 = (f32[38912]{0:T(1024)S(1)}, f32[38912]{0:T(1024)S(1)}, u32[]{:S(2)}, u32[]{:S(2)}) collective-permute-start(f32[38912]{0:T(1024)S(1)} %pad_maximum_fusion.6), channel_id=1, source_target_pairs={{1,0},{2,1},{3,2},{4,3},{5,4},{6,5},{7,6},{9,8},{10,9},{11,10},{12... | collective-permute-start | bytes 466952 | tf_op jit(solution)/shard_map/ppermute | solution.py:17
  41.2 0.8 reshape.718.x_lo_ref
  42.0 0.8 reshape.721.x_hi_ref
  42.8 5.0 %collective-permute-done.3 = f32[38912]{0:T(1024)S(1)} collective-permute-done((f32[38912]{0:T(1024)S(1)}, f32[38912]{0:T(1024)S(1)}, u32[]{:S(2)}, u32[]{:S(2)}) %collective-permute-start.3) | collective-permute-done | bytes 155680 | tf_op jit(solution)/shard_map/ppermute | solution.py:17
  49.1 0.7 slice.290
  49.7 0.7 slice.289
  50.4 6.7 %shard_map.193 = (f32[4,8,16,1024]{3,2,1,0:T(8,128)}, f32[4,16,1024]{2,1,0:T(8,128)}, f32[4,8,1024]{2,1,0:T(8,128)}, f32[4,1024]{1,0:T(4,128)}, f32[640,1024]{1,0:T(8,128)}) custom-call(f32[4,8,16,1024]{3,2,1,0:T(8,128)} %state_ref.1, f32[4,1,16,1024]{3,2,1,0:T(8,128)} %reshape.718.x_lo_ref, f32[4,1,16,1024]{3,2,1,0:T(8,128)} %reshape.721.x_hi_ref, ...), custom_call_target="tpu_custom_call" | custom-call | tf_op jit(solution)/shard_map/pallas_call | solution.py:75
  57.1 3.6 %collective-permute-start.4 = (f32[4,16,1024]{2,1,0:T(8,128)}, f32[4,16,1024]{2,1,0:T(8,128)S(1)}, u32[]{:S(2)}, u32[]{:S(2)}) collective-permute-start(f32[4,16,1024]{2,1,0:T(8,128)} %get-tuple-element.10), channel_id=1, source_target_pairs={{8,0},{16,8},{24,16},{32,24},{40,32},{48,40},{56,48},{64,56},{72,6... | collective-permute-start | bytes 786440 | tf_op jit(solution)/shard_map/ppermute | solution.py:17
  60.7 1.3 %collective-permute-start.5 = (f32[4,8,1024]{2,1,0:T(8,128)}, f32[4,8,1024]{2,1,0:T(8,128)S(1)}, u32[]{:S(2)}, u32[]{:S(2)}) collective-permute-start(f32[4,8,1024]{2,1,0:T(8,128)} %get-tuple-element.11), channel_id=1, source_target_pairs={{1,0},{2,1},{3,2},{4,3},{5,4},{6,5},{7,6},{9,8},{10,9},{11,10},{12... | collective-permute-start | bytes 393224 | tf_op jit(solution)/shard_map/ppermute | solution.py:17
  62.0 1.5 %collective-permute-start.6 = (f32[4,1024]{1,0:T(4,128)}, f32[4,1024]{1,0:T(4,128)S(1)}, u32[]{:S(2)}, u32[]{:S(2)}) collective-permute-start(f32[4,1024]{1,0:T(4,128)} %get-tuple-element.12), channel_id=1, source_target_pairs={{9,0},{10,1},{11,2},{12,3},{13,4},{14,5},{15,6},{17,8},{18,9},{19,... | collective-permute-start | bytes 49160 | tf_op jit(solution)/shard_map/ppermute | solution.py:112
  63.7 20.8 %multiply_reduce_fusion.2 = (f32[16,128]{1,0:T(8,128)S(1)}, f32[16,128]{1,0:T(8,128)S(1)}, f32[16,128]{1,0:T(8,128)S(1)}, f32[16,128]{1,0:T(8,128)S(1)}, f32[16,...) fusion(f32[16,1152]{1,0:T(8,128)S(1)} %get-tuple-element.82, f32[16,1152]{1,0:T(8,128)S(1)} %get-tuple-element.83, ...), kind=kLoop, calls=%fused_computation.18 | loop fusion | flops 68405248 | bytes 679936 | tf_op jit(solution)/shard_map/reduce_sum | solution.py:165
  84.7 1.8 %dynamic_update_slice.3 = f32[640,1024]{1,0:T(8,128)} dynamic-update-slice(f32[640,1024]{1,0:T(8,128)} %get-tuple-element.9, f32[100,1024]{1,0:T(8,128)S(1)} %reshape.728, s32[]{:T(128)} %constant.75.clone.1, s32[]{:T(128)} %constant.76.clone.1) | dynamic-update-slice | bytes 819204 | tf_op jit(solution)/shard_map/dynamic_update_slice | solution.py:238
  86.6 10.5 %fusion.9 = f32[640,2048]{1,0:T(8,128)S(1)} fusion(f32[640,1024]{1,0:T(8,128)} %dynamic_update_slice.3, f32[2048]{0:T(1024)S(1)} %slice.247, s32[2048]{0:T(1024)S(1)} %get-tuple-element.75, f32[2048]{0:T(1024)S(1)} %broadcast_subtract_fusion.2, s32[2048]{0:T(1024)S(1)} %get-tuple-element.76), kind=kOutput, calls=%fused_computation.20 | convolution fusion | flops 8063549440 | bytes 7897088 | tf_op jit(solution)/shard_map/dot_general | solution.py:127
  97.1 0.6 fusion.29
  97.7 0.2 fusion.35
  98.1 0.1 add.351
  98.2 0.1 add.353
  98.4 0.1 add.355
  98.6 0.7 copy.88
  99.3 8.8 %all-to-all-start.1 = ((f32[128,1,64]{2,1,0:T(1,128)}), f32[128,1,64]{2,1,0:T(1,128)S(1)}, u32[]{:S(2)}, u32[]{:S(2)}) async-start(f32[128,1,64]{2,1,0:T(1,128)} %copy.88), calls=%async_computation.1 | async-start | bytes 131072 | tf_op jit(solution)/shard_map/all_to_all | solution.py:90
  108.1 0.6 maximum_multiply_fusion
  108.7 8.9 %all-to-all-done.1 = f32[128,1,64]{2,1,0:T(1,128)S(1)} async-done(((f32[128,1,64]{2,1,0:T(1,128)}), f32[128,1,64]{2,1,0:T(1,128)S(1)}, u32[]{:S(2)}, u32[]{:S(2)}) %all-to-all-start.1) | async-done | bytes 32800 | tf_op jit(solution)/shard_map/all_to_all | solution.py:90
  117.7 0.1 copy.90
  117.8 0.2 reshape.732
  118.0 1.7 %fusion.13 = f32[12,1024]{1,0:T(8,128)S(1)} fusion(s32[1024]{0:T(1024)S(1)} %bitcast.183, bf16[4,2048]{1,0:T(4,128)(2,1)S(1)} %get-tuple-element.55, bf16[4,2048]{1,0:T(4,128)(2,1)S(1)} %get-tuple-element.56, bf16[4,2048]{1,0:T(4,128)(2,1)S(1)} %get-tuple-element.54), kind=kOutput, calls=%fused_computation.26 | convolution fusion | flops 52576256 | bytes 102400 | tf_op jit(solution)/shard_map/dot_general | solution.py:243
  119.7 0.6 fusion.68
  (109 shorter events, 2.9 us)
Async XLA Ops:
  0.6 27.7 %copy-start.4 = (s32[4,4]{1,0:T(4,128)S(1)}, s32[4,4]{1,0:T(4,128)}, u32[]{:S(2)}) copy-start(s32[4,4]{1,0:T(4,128)} %param.26) | copy-start | bytes 196
  0.6 27.7 %copy-start = (f32[3,4,4,128]{3,2,1,0:T(4,128)S(1)}, f32[3,4,4,128]{3,2,1,0:T(4,128)}, u32[]{:S(2)}) copy-start(f32[3,4,4,128]{3,2,1,0:T(4,128)} %param.23) | copy-start | bytes 73732
  0.7 11.4 %copy-start.5 = (s32[1024,1]{0,1:T(1,128)S(1)}, s32[1024,1]{0,1:T(1,128)}, u32[]{:S(2)}) copy-start(s32[1024,1]{0,1:T(1,128)} %param.19) | copy-start | bytes 12292
  0.7 11.4 %copy-start.6 = (s32[1024]{0:T(1024)S(1)}, s32[1024]{0:T(1024)}, u32[]{:S(2)}) copy-start(s32[1024]{0:T(1024)} %param.20) | copy-start | bytes 12292
  0.7 11.4 %copy-start.3 = (f32[3,1024]{1,0:T(4,128)S(1)}, f32[3,1024]{1,0:T(4,128)}, u32[]{:S(2)}) copy-start(f32[3,1024]{1,0:T(4,128)} %param.21) | copy-start | bytes 36868
  3.4 34.0 %collective-permute-start = (f32[69632]{0:T(1024)S(1)}, f32[69632]{0:T(1024)S(1)}, u32[]{:S(2)}, u32[]{:S(2)}) collective-permute-start(f32[69632]{0:T(1024)S(1)} %pad_maximum_fusion.1), channel_id=1, source_target_pairs={{0,8},{8,16},{16,24},{24,32},{32,40},{40,48},{48,56},{56,64},{64,7... | collective-permute-start | bytes 835592 | tf_op jit(solution)/shard_map/ppermute | solution.py:17
  7.9 29.6 %copy-start.1 = (f32[3,4,4,128]{3,2,1,0:T(4,128)S(1)}, f32[3,4,4,128]{3,2,1,0:T(4,128)}, u32[]{:S(2)}) copy-start(f32[3,4,4,128]{3,2,1,0:T(4,128)} %param.24) | copy-start | bytes 73732
  7.9 29.6 %copy-start.2 = (f32[4,4,128]{2,1,0:T(4,128)S(1)}, f32[4,4,128]{2,1,0:T(4,128)}, u32[]{:S(2)}) copy-start(f32[4,4,128]{2,1,0:T(4,128)} %param.25) | copy-start | bytes 24580
  8.0 29.4 %collective-permute-start.1 = (f32[69632]{0:T(1024)S(1)}, f32[69632]{0:T(1024)S(1)}, u32[]{:S(2)}, u32[]{:S(2)}) collective-permute-start(f32[69632]{0:T(1024)S(1)} %pad_maximum_fusion.2), channel_id=1, source_target_pairs={{8,0},{16,8},{24,16},{32,24},{40,32},{48,40},{56,48},{64,56},{72,6... | collective-permute-start | bytes 835592 | tf_op jit(solution)/shard_map/ppermute | solution.py:17
  12.0 35.9 %copy-start.11 = (f32[8]{0:T(128)S(1)}, f32[8]{0:T(128)}, u32[]{:S(2)}) copy-start(f32[8]{0:T(128)} %constant.93.clone) | copy-start | bytes 100
  12.1 35.9 %copy-start.14 = (f32[8]{0:T(128)S(1)}, f32[8]{0:T(128)}, u32[]{:S(2)}) copy-start(f32[8]{0:T(128)} %constant.94.clone) | copy-start | bytes 100
  12.1 36.0 %copy-start.13 = (f32[8]{0:T(128)S(1)}, f32[8]{0:T(128)}, u32[]{:S(2)}) copy-start(f32[8]{0:T(128)} %constant.95.clone) | copy-start | bytes 100
  12.2 36.0 %copy-start.12 = (f32[8]{0:T(128)S(1)}, f32[8]{0:T(128)}, u32[]{:S(2)}) copy-start(f32[8]{0:T(128)} %constant.96.clone) | copy-start | bytes 100
  12.2 36.2 %copy-start.10 = (f32[8]{0:T(128)S(1)}, f32[8]{0:T(128)}, u32[]{:S(2)}) copy-start(f32[8]{0:T(128)} %constant.98.clone) | copy-start | bytes 100
  12.2 36.2 %copy-start.9 = (f32[8]{0:T(128)S(1)}, f32[8]{0:T(128)}, u32[]{:S(2)}) copy-start(f32[8]{0:T(128)} %constant.99.clone) | copy-start | bytes 100
  12.2 36.3 %copy-start.8 = (f32[8]{0:T(128)S(1)}, f32[8]{0:T(128)}, u32[]{:S(2)}) copy-start(f32[8]{0:T(128)} %constant.100.clone) | copy-start | bytes 100
  12.2 36.4 %copy-start.7 = (f32[8]{0:T(128)S(1)}, f32[8]{0:T(128)}, u32[]{:S(2)}) copy-start(f32[8]{0:T(128)} %constant.101.clone) | copy-start | bytes 100
  14.8 21.2 %all-to-all-start = ((f32[128,1,64]{2,1,0:T(1,128)}), f32[128,1,64]{2,1,0:T(1,128)S(1)}, u32[]{:S(2)}, u32[]{:S(2)}) async-start(f32[128,1,64]{2,1,0:T(1,128)} %copy.75), calls=%async_computation | async-start | bytes 131072 | tf_op jit(solution)/shard_map/all_to_all | solution.py:90
  37.6 5.2 %collective-permute-start.2 = (f32[38912]{0:T(1024)S(1)}, f32[38912]{0:T(1024)S(1)}, u32[]{:S(2)}, u32[]{:S(2)}) collective-permute-start(f32[38912]{0:T(1024)S(1)} %pad_maximum_fusion.5), channel_id=1, source_target_pairs={{0,1},{1,2},{2,3},{3,4},{4,5},{5,6},{6,7},{8,9},{9,10},{10,11},{11... | collective-permute-start | bytes 466952 | tf_op jit(solution)/shard_map/ppermute | solution.py:17
  39.9 7.9 %collective-permute-start.3 = (f32[38912]{0:T(1024)S(1)}, f32[38912]{0:T(1024)S(1)}, u32[]{:S(2)}, u32[]{:S(2)}) collective-permute-start(f32[38912]{0:T(1024)S(1)} %pad_maximum_fusion.6), channel_id=1, source_target_pairs={{1,0},{2,1},{3,2},{4,3},{5,4},{6,5},{7,6},{9,8},{10,9},{11,10},{12... | collective-permute-start | bytes 466952 | tf_op jit(solution)/shard_map/ppermute | solution.py:17
  57.1 27.5 %collective-permute-start.4 = (f32[4,16,1024]{2,1,0:T(8,128)}, f32[4,16,1024]{2,1,0:T(8,128)S(1)}, u32[]{:S(2)}, u32[]{:S(2)}) collective-permute-start(f32[4,16,1024]{2,1,0:T(8,128)} %get-tuple-element.10), channel_id=1, source_target_pairs={{8,0},{16,8},{24,16},{32,24},{40,32},{48,40},{56,48},{64,56},{72,6... | collective-permute-start | bytes 786440 | tf_op jit(solution)/shard_map/ppermute | solution.py:17
  60.7 23.9 %collective-permute-start.5 = (f32[4,8,1024]{2,1,0:T(8,128)}, f32[4,8,1024]{2,1,0:T(8,128)S(1)}, u32[]{:S(2)}, u32[]{:S(2)}) collective-permute-start(f32[4,8,1024]{2,1,0:T(8,128)} %get-tuple-element.11), channel_id=1, source_target_pairs={{1,0},{2,1},{3,2},{4,3},{5,4},{6,5},{7,6},{9,8},{10,9},{11,10},{12... | collective-permute-start | bytes 393224 | tf_op jit(solution)/shard_map/ppermute | solution.py:17
  62.0 22.6 %collective-permute-start.6 = (f32[4,1024]{1,0:T(4,128)}, f32[4,1024]{1,0:T(4,128)S(1)}, u32[]{:S(2)}, u32[]{:S(2)}) collective-permute-start(f32[4,1024]{1,0:T(4,128)} %get-tuple-element.12), channel_id=1, source_target_pairs={{9,0},{10,1},{11,2},{12,3},{13,4},{14,5},{15,6},{17,8},{18,9},{19,... | collective-permute-start | bytes 49160 | tf_op jit(solution)/shard_map/ppermute | solution.py:112
  99.3 18.3 %all-to-all-start.1 = ((f32[128,1,64]{2,1,0:T(1,128)}), f32[128,1,64]{2,1,0:T(1,128)S(1)}, u32[]{:S(2)}, u32[]{:S(2)}) async-start(f32[128,1,64]{2,1,0:T(1,128)} %copy.88), calls=%async_computation.1 | async-start | bytes 131072 | tf_op jit(solution)/shard_map/all_to_all | solution.py:90

commit v4 on v3

--- a/solution.py
+++ b/solution.py
@@ -92,12 +92,14 @@
 
 
 def packed_permute(arrays, axis, by):
-    flat = jnp.concatenate([array.reshape(-1) for array in arrays])
+    width = arrays[0].shape[-1]
+    flat = jnp.concatenate([array.reshape(-1, width) for array in arrays], axis=0)
     moved = from_behind(flat, axis, by)
     parts, offset = [], 0
     for array in arrays:
-        parts.append(moved[offset : offset + array.size].reshape(array.shape))
-        offset += array.size
+        rows = array.size // width
+        parts.append(moved[offset : offset + rows].reshape(array.shape))
+        offset += rows
     return parts
 
 

time: 121 us -> 124 us (1.025)
  other arithmetic: 25.9 us -> 28.1 us
  transfers between devices with their start and end apart: 9 -> 9, of which waited for: 3 -> 3; matrix products, arithmetic and copies ran while one was open for 25% -> 27% of each run, Pallas kernels for 0% -> 0%
where the time goes in v4:
time: 124 us; the launch traced here: 123 us
  starting transfers between devices  37 us (30%)
  other arithmetic  28.1 us (23%)
  waiting for transfers between devices  21.6 us (17%)
  matrix products  15.3 us (12%)
  local copies, waits for them, and re-layouts  12.3 us (10%)
  Pallas kernels  6.65 us (5%)
  between operations  2.09 us (2%)
    reduce_sum x1, other arithmetic, pair_sums(): jnp.sum(weight * other_tiles[3 + channel][:, :, None], axis=1)  20.8 us
    all_to_all x2, starting transfers between devices, exchange(): lax.all_to_all(rows.reshape(devices, -1), ('gx', 'gy'), 0, 0, tiled=True)  20.5 us
    all_to_all x2, waiting for transfers between devices, exchange(): lax.all_to_all(rows.reshape(devices, -1), ('gx', 'gy'), 0, 0, tiled=True)  16.3 us
    ppermute x6, starting transfers between devices, from_behind(): return lax.ppermute(array, axis, pairs)  15 us
    dot_general x1, matrix products, answer_requests(): lax.dot_general(table, z_weight, (((1,), (0,)), ((), ())), precision=lax....  10.7 us
    pallas_call x1, Pallas kernels, flux_sweep(): pl.pallas_call(flux_kernel, out_shape=(jax.ShapeDtypeStruct(state.shape,...  6.65 us
    ppermute x6, waiting for transfers between devices, from_behind(): return lax.ppermute(array, axis, pairs)  5.31 us
  transfers between devices with their start and end apart: 9, of which 3 were waited for; matrix products, arithmetic and copies ran while one was open for 27% of the time, Pallas kernels for 0%

profile of v4, /device:TPU:1, one launch (start us, length us, event | category | flops | bytes accessed | tf_op | source)
XLA Modules:
  0.0 123.2 jit_solution(18098085211935176724)
XLA Ops:
  0.7 0.8 fusion.79
  1.5 0.8 pad_maximum_fusion.21
  2.3 1.1 fusion.84
  3.4 4.5 %collective-permute-start = (f32[68,1024]{1,0:T(8,128)S(1)}, f32[68,1024]{1,0:T(8,128)S(1)}, u32[]{:S(2)}, u32[]{:S(2)}) collective-permute-start(f32[68,1024]{1,0:T(8,128)S(1)} %pad_maximum_fusion.1), channel_id=1, source_target_pairs={{0,8},{8,16},{16,24},{24,32},{32,40},{40,48},{48,56},{56,64},{64,7... | collective-permute-start | bytes 835592 | tf_op jit(solution)/shard_map/ppermute | solution.py:17
  7.9 1.9 %collective-permute-start.1 = (f32[68,1024]{1,0:T(8,128)S(1)}, f32[68,1024]{1,0:T(8,128)S(1)}, u32[]{:S(2)}, u32[]{:S(2)}) collective-permute-start(f32[68,1024]{1,0:T(8,128)S(1)} %pad_maximum_fusion.2), channel_id=1, source_target_pairs={{8,0},{16,8},{24,16},{32,24},{40,32},{48,40},{56,48},{64,56},{72,6... | collective-permute-start | bytes 835592 | tf_op jit(solution)/shard_map/ppermute | solution.py:17
  10.5 1.4 %fusion.25 = f32[1024]{0:T(1024)S(1)} fusion(s32[1024]{0:T(1024)} %bitcast.161, pred[1024]{0:T(1024)(128)(4,1)S(1)} %iota_compare_fusion.20), kind=kOutput, calls=%fused_computation.40 | convolution fusion | flops 270269440 | bytes 9216 | tf_op jit(solution)/shard_map/dot_general | solution.py:222
  12.0 0.7 convert_element_type.83
  12.7 0.7 compare_select_fusion.4
  13.4 0.7 reduce-precision_convert_fusion.3
  14.2 1.6 %fusion.14 = f32[12,2048]{1,0:T(8,128)S(1)} fusion(s32[1024]{0:T(1024)S(1)} %bitcast.162, bf16[4,1024]{1,0:T(4,128)(2,1)S(1)} %get-tuple-element.70, bf16[4,1024]{1,0:T(4,128)(2,1)S(1)} %get-tuple-element.69, bf16[4,1024]{1,0:T(4,128)(2,1)S(1)} %get-tuple-element.68), kind=kOutput, calls=%fused_computation.27 | convolution fusion | flops 52502528 | bytes 126976 | tf_op jit(solution)/shard_map/dot_general | solution.py:230
  15.8 0.1 reshape.719
  16.0 0.7 copy.110
  16.7 11.8 %all-to-all-start = ((f32[128,1,64]{2,1,0:T(1,128)}), f32[128,1,64]{2,1,0:T(1,128)S(1)}, u32[]{:S(2)}, u32[]{:S(2)}) async-start(f32[128,1,64]{2,1,0:T(1,128)} %copy.110), calls=%async_computation | async-start | bytes 131072 | tf_op jit(solution)/shard_map/all_to_all | solution.py:90
  28.5 1.8 %fusion.83 = (f32[4,8,1,1024]{3,2,1,0:T(1,128)S(1)}, f32[4,8,1,1024]{3,2,1,0:T(1,128)S(1)}) fusion(f32[4,8,16,1024]{3,2,1,0:T(8,128)} %state_ref.1), kind=kLoop, calls=%fused_computation.213 | loop fusion | bytes 524288 | tf_op jit(solution)/shard_map/slice | solution.py:208
  30.5 7.5 %all-to-all-done = f32[128,1,64]{2,1,0:T(1,128)S(1)} async-done(((f32[128,1,64]{2,1,0:T(1,128)}), f32[128,1,64]{2,1,0:T(1,128)S(1)}, u32[]{:S(2)}, u32[]{:S(2)}) %all-to-all-start) | async-done | bytes 32800 | tf_op jit(solution)/shard_map/all_to_all | solution.py:90
  38.0 0.1 copy.112
  38.3 0.1 copy.114
  38.6 0.1 copy.115
  38.9 0.1 copy.113
  39.3 0.1 fusion.72
  39.5 0.1 fusion.67
  39.7 2.3 %collective-permute-start.2 = (f32[38,1024]{1,0:T(8,128)S(1)}, f32[38,1024]{1,0:T(8,128)S(1)}, u32[]{:S(2)}, u32[]{:S(2)}) collective-permute-start(f32[38,1024]{1,0:T(8,128)S(1)} %pad_maximum_fusion.5), channel_id=1, source_target_pairs={{0,1},{1,2},{2,3},{3,4},{4,5},{5,6},{6,7},{8,9},{9,10},{10,11},{11... | collective-permute-start | bytes 466952 | tf_op jit(solution)/shard_map/ppermute | solution.py:17
  42.0 1.3 %collective-permute-start.3 = (f32[38,1024]{1,0:T(8,128)S(1)}, f32[38,1024]{1,0:T(8,128)S(1)}, u32[]{:S(2)}, u32[]{:S(2)}) collective-permute-start(f32[38,1024]{1,0:T(8,128)S(1)} %pad_maximum_fusion.6), channel_id=1, source_target_pairs={{1,0},{2,1},{3,2},{4,3},{5,4},{6,5},{7,6},{9,8},{10,9},{11,10},{12... | collective-permute-start | bytes 466952 | tf_op jit(solution)/shard_map/ppermute | solution.py:17
  43.3 0.7 slice.263
  44.0 0.7 slice.264
  44.8 5.3 %collective-permute-done.3 = f32[38,1024]{1,0:T(8,128)S(1)} collective-permute-done((f32[38,1024]{1,0:T(8,128)S(1)}, f32[38,1024]{1,0:T(8,128)S(1)}, u32[]{:S(2)}, u32[]{:S(2)}) %collective-permute-start.3) | collective-permute-done | bytes 155680 | tf_op jit(solution)/shard_map/ppermute | solution.py:17
  51.4 0.8 reshape.714.y_lo_ref
  52.3 0.8 reshape.717.y_hi_ref
  53.1 6.7 %shard_map.193 = (f32[4,8,16,1024]{3,2,1,0:T(8,128)}, f32[4,16,1024]{2,1,0:T(8,128)}, f32[4,8,1024]{2,1,0:T(8,128)}, f32[4,1024]{1,0:T(4,128)}, f32[640,1024]{1,0:T(8,128)}) custom-call(f32[4,8,16,1024]{3,2,1,0:T(8,128)} %state_ref.1, f32[4,1,16,1024]{3,2,1,0:T(8,128)} %bitcast.125, f32[4,1,16,1024]{3,2,1,0:T(8,128)} %bitcast.126, ...), custom_call_target="tpu_custom_call" | custom-call | tf_op jit(solution)/shard_map/pallas_call | solution.py:75
  59.7 3.8 %collective-permute-start.4 = (f32[4,16,1024]{2,1,0:T(8,128)}, f32[4,16,1024]{2,1,0:T(8,128)S(1)}, u32[]{:S(2)}, u32[]{:S(2)}) collective-permute-start(f32[4,16,1024]{2,1,0:T(8,128)} %get-tuple-element.10), channel_id=1, source_target_pairs={{8,0},{16,8},{24,16},{32,24},{40,32},{48,40},{56,48},{64,56},{72,6... | collective-permute-start | bytes 786440 | tf_op jit(solution)/shard_map/ppermute | solution.py:17
  63.5 1.3 %collective-permute-start.5 = (f32[4,8,1024]{2,1,0:T(8,128)}, f32[4,8,1024]{2,1,0:T(8,128)S(1)}, u32[]{:S(2)}, u32[]{:S(2)}) collective-permute-start(f32[4,8,1024]{2,1,0:T(8,128)} %get-tuple-element.11), channel_id=1, source_target_pairs={{1,0},{2,1},{3,2},{4,3},{5,4},{6,5},{7,6},{9,8},{10,9},{11,10},{12... | collective-permute-start | bytes 393224 | tf_op jit(solution)/shard_map/ppermute | solution.py:17
  64.8 1.5 %collective-permute-start.6 = (f32[4,1024]{1,0:T(4,128)}, f32[4,1024]{1,0:T(4,128)S(1)}, u32[]{:S(2)}, u32[]{:S(2)}) collective-permute-start(f32[4,1024]{1,0:T(4,128)} %get-tuple-element.12), channel_id=1, source_target_pairs={{9,0},{10,1},{11,2},{12,3},{13,4},{14,5},{15,6},{17,8},{18,9},{19,... | collective-permute-start | bytes 49160 | tf_op jit(solution)/shard_map/ppermute | solution.py:114
  66.5 20.8 %multiply_reduce_fusion.2 = (f32[16,128]{1,0:T(8,128)S(1)}, f32[16,128]{1,0:T(8,128)S(1)}, f32[16,128]{1,0:T(8,128)S(1)}, f32[16,128]{1,0:T(8,128)S(1)}, f32[16,...) fusion(f32[16,1152]{1,0:T(8,128)S(1)} %get-tuple-element.82, f32[16,1152]{1,0:T(8,128)S(1)} %get-tuple-element.83, ...), kind=kLoop, calls=%fused_computation.18 | loop fusion | flops 68405248 | bytes 679936 | tf_op jit(solution)/shard_map/reduce_sum | solution.py:167
  87.5 1.8 %dynamic_update_slice.3 = f32[640,1024]{1,0:T(8,128)} dynamic-update-slice(f32[640,1024]{1,0:T(8,128)} %get-tuple-element.9, f32[100,1024]{1,0:T(8,128)S(1)} %reshape.718, s32[]{:T(128)} %constant.75.clone.1, s32[]{:T(128)} %constant.76.clone.1) | dynamic-update-slice | bytes 819204 | tf_op jit(solution)/shard_map/dynamic_update_slice | solution.py:240
  89.4 10.7 %fusion.9 = f32[640,2048]{1,0:T(8,128)S(1)} fusion(f32[640,1024]{1,0:T(8,128)} %dynamic_update_slice.3, f32[2048]{0:T(1024)S(1)} %slice.225, s32[2048]{0:T(1024)S(1)} %get-tuple-element.75, f32[2048]{0:T(1024)S(1)} %broadcast_subtract_fusion.2, s32[2048]{0:T(1024)S(1)} %get-tuple-element.76), kind=kOutput, calls=%fused_computation.20 | convolution fusion | flops 8063549440 | bytes 7897088 | tf_op jit(solution)/shard_map/dot_general | solution.py:129
  100.1 0.6 fusion.29
  100.7 0.2 fusion.35
  101.0 0.1 add.351
  101.2 0.1 add.353
  101.4 0.1 add.355
  101.5 0.7 copy.123
  102.3 8.7 %all-to-all-start.1 = ((f32[128,1,64]{2,1,0:T(1,128)}), f32[128,1,64]{2,1,0:T(1,128)S(1)}, u32[]{:S(2)}, u32[]{:S(2)}) async-start(f32[128,1,64]{2,1,0:T(1,128)} %copy.123), calls=%async_computation.1 | async-start | bytes 131072 | tf_op jit(solution)/shard_map/all_to_all | solution.py:90
  111.0 0.6 maximum_multiply_fusion
  111.6 8.9 %all-to-all-done.1 = f32[128,1,64]{2,1,0:T(1,128)S(1)} async-done(((f32[128,1,64]{2,1,0:T(1,128)}), f32[128,1,64]{2,1,0:T(1,128)S(1)}, u32[]{:S(2)}, u32[]{:S(2)}) %all-to-all-start.1) | async-done | bytes 32800 | tf_op jit(solution)/shard_map/all_to_all | solution.py:90
  120.5 0.1 copy.125
  120.7 0.2 reshape.722
  120.9 1.7 %fusion.13 = f32[12,1024]{1,0:T(8,128)S(1)} fusion(s32[1024]{0:T(1024)S(1)} %bitcast.163, bf16[4,2048]{1,0:T(4,128)(2,1)S(1)} %get-tuple-element.55, bf16[4,2048]{1,0:T(4,128)(2,1)S(1)} %get-tuple-element.56, bf16[4,2048]{1,0:T(4,128)(2,1)S(1)} %get-tuple-element.54), kind=kOutput, calls=%fused_computation.26 | convolution fusion | flops 52576256 | bytes 102400 | tf_op jit(solution)/shard_map/dot_general | solution.py:245
  122.6 0.6 fusion.69
  (111 shorter events, 3.3 us)
Async XLA Ops:
  0.6 29.7 %copy-start.3 = (s32[4,4]{1,0:T(4,128)S(1)}, s32[4,4]{1,0:T(4,128)}, u32[]{:S(2)}) copy-start(s32[4,4]{1,0:T(4,128)} %param.26) | copy-start | bytes 196
  0.6 29.7 %copy-start = (f32[3,4,4,128]{3,2,1,0:T(4,128)S(1)}, f32[3,4,4,128]{3,2,1,0:T(4,128)}, u32[]{:S(2)}) copy-start(f32[3,4,4,128]{3,2,1,0:T(4,128)} %param.23) | copy-start | bytes 73732
  3.4 36.0 %collective-permute-start = (f32[68,1024]{1,0:T(8,128)S(1)}, f32[68,1024]{1,0:T(8,128)S(1)}, u32[]{:S(2)}, u32[]{:S(2)}) collective-permute-start(f32[68,1024]{1,0:T(8,128)S(1)} %pad_maximum_fusion.1), channel_id=1, source_target_pairs={{0,8},{8,16},{16,24},{24,32},{32,40},{40,48},{48,56},{56,64},{64,7... | collective-permute-start | bytes 835592 | tf_op jit(solution)/shard_map/ppermute | solution.py:17
  7.9 31.6 %copy-start.1 = (f32[3,4,4,128]{3,2,1,0:T(4,128)S(1)}, f32[3,4,4,128]{3,2,1,0:T(4,128)}, u32[]{:S(2)}) copy-start(f32[3,4,4,128]{3,2,1,0:T(4,128)} %param.24) | copy-start | bytes 73732
  7.9 31.6 %copy-start.2 = (f32[4,4,128]{2,1,0:T(4,128)S(1)}, f32[4,4,128]{2,1,0:T(4,128)}, u32[]{:S(2)}) copy-start(f32[4,4,128]{2,1,0:T(4,128)} %param.25) | copy-start | bytes 24580
  7.9 31.5 %collective-permute-start.1 = (f32[68,1024]{1,0:T(8,128)S(1)}, f32[68,1024]{1,0:T(8,128)S(1)}, u32[]{:S(2)}, u32[]{:S(2)}) collective-permute-start(f32[68,1024]{1,0:T(8,128)S(1)} %pad_maximum_fusion.2), channel_id=1, source_target_pairs={{8,0},{16,8},{24,16},{32,24},{40,32},{48,40},{56,48},{64,56},{72,6... | collective-permute-start | bytes 835592 | tf_op jit(solution)/shard_map/ppermute | solution.py:17
  11.9 38.3 %copy-start.8 = (f32[8]{0:T(128)S(1)}, f32[8]{0:T(128)}, u32[]{:S(2)}) copy-start(f32[8]{0:T(128)} %constant.93.clone) | copy-start | bytes 100
  11.9 38.4 %copy-start.11 = (f32[8]{0:T(128)S(1)}, f32[8]{0:T(128)}, u32[]{:S(2)}) copy-start(f32[8]{0:T(128)} %constant.94.clone) | copy-start | bytes 100
  14.1 36.3 %copy-start.10 = (f32[8]{0:T(128)S(1)}, f32[8]{0:T(128)}, u32[]{:S(2)}) copy-start(f32[8]{0:T(128)} %constant.95.clone) | copy-start | bytes 100
  14.1 36.4 %copy-start.9 = (f32[8]{0:T(128)S(1)}, f32[8]{0:T(128)}, u32[]{:S(2)}) copy-start(f32[8]{0:T(128)} %constant.96.clone) | copy-start | bytes 100
  14.1 36.6 %copy-start.7 = (f32[8]{0:T(128)S(1)}, f32[8]{0:T(128)}, u32[]{:S(2)}) copy-start(f32[8]{0:T(128)} %constant.98.clone) | copy-start | bytes 100
  14.1 36.6 %copy-start.6 = (f32[8]{0:T(128)S(1)}, f32[8]{0:T(128)}, u32[]{:S(2)}) copy-start(f32[8]{0:T(128)} %constant.99.clone) | copy-start | bytes 100
  14.2 36.7 %copy-start.5 = (f32[8]{0:T(128)S(1)}, f32[8]{0:T(128)}, u32[]{:S(2)}) copy-start(f32[8]{0:T(128)} %constant.100.clone) | copy-start | bytes 100
  14.2 36.8 %copy-start.4 = (f32[8]{0:T(128)S(1)}, f32[8]{0:T(128)}, u32[]{:S(2)}) copy-start(f32[8]{0:T(128)} %constant.101.clone) | copy-start | bytes 100
  16.7 21.2 %all-to-all-start = ((f32[128,1,64]{2,1,0:T(1,128)}), f32[128,1,64]{2,1,0:T(1,128)S(1)}, u32[]{:S(2)}, u32[]{:S(2)}) async-start(f32[128,1,64]{2,1,0:T(1,128)} %copy.110), calls=%async_computation | async-start | bytes 131072 | tf_op jit(solution)/shard_map/all_to_all | solution.py:90
  39.7 5.1 %collective-permute-start.2 = (f32[38,1024]{1,0:T(8,128)S(1)}, f32[38,1024]{1,0:T(8,128)S(1)}, u32[]{:S(2)}, u32[]{:S(2)}) collective-permute-start(f32[38,1024]{1,0:T(8,128)S(1)} %pad_maximum_fusion.5), channel_id=1, source_target_pairs={{0,1},{1,2},{2,3},{3,4},{4,5},{5,6},{6,7},{8,9},{9,10},{10,11},{11... | collective-permute-start | bytes 466952 | tf_op jit(solution)/shard_map/ppermute | solution.py:17
  42.0 8.1 %collective-permute-start.3 = (f32[38,1024]{1,0:T(8,128)S(1)}, f32[38,1024]{1,0:T(8,128)S(1)}, u32[]{:S(2)}, u32[]{:S(2)}) collective-permute-start(f32[38,1024]{1,0:T(8,128)S(1)} %pad_maximum_fusion.6), channel_id=1, source_target_pairs={{1,0},{2,1},{3,2},{4,3},{5,4},{6,5},{7,6},{9,8},{10,9},{11,10},{12... | collective-permute-start | bytes 466952 | tf_op jit(solution)/shard_map/ppermute | solution.py:17
  59.7 27.7 %collective-permute-start.4 = (f32[4,16,1024]{2,1,0:T(8,128)}, f32[4,16,1024]{2,1,0:T(8,128)S(1)}, u32[]{:S(2)}, u32[]{:S(2)}) collective-permute-start(f32[4,16,1024]{2,1,0:T(8,128)} %get-tuple-element.10), channel_id=1, source_target_pairs={{8,0},{16,8},{24,16},{32,24},{40,32},{48,40},{56,48},{64,56},{72,6... | collective-permute-start | bytes 786440 | tf_op jit(solution)/shard_map/ppermute | solution.py:17
  63.5 23.9 %collective-permute-start.5 = (f32[4,8,1024]{2,1,0:T(8,128)}, f32[4,8,1024]{2,1,0:T(8,128)S(1)}, u32[]{:S(2)}, u32[]{:S(2)}) collective-permute-start(f32[4,8,1024]{2,1,0:T(8,128)} %get-tuple-element.11), channel_id=1, source_target_pairs={{1,0},{2,1},{3,2},{4,3},{5,4},{6,5},{7,6},{9,8},{10,9},{11,10},{12... | collective-permute-start | bytes 393224 | tf_op jit(solution)/shard_map/ppermute | solution.py:17
  64.8 22.6 %collective-permute-start.6 = (f32[4,1024]{1,0:T(4,128)}, f32[4,1024]{1,0:T(4,128)S(1)}, u32[]{:S(2)}, u32[]{:S(2)}) collective-permute-start(f32[4,1024]{1,0:T(4,128)} %get-tuple-element.12), channel_id=1, source_target_pairs={{9,0},{10,1},{11,2},{12,3},{13,4},{14,5},{15,6},{17,8},{18,9},{19,... | collective-permute-start | bytes 49160 | tf_op jit(solution)/shard_map/ppermute | solution.py:114
  102.3 18.2 %all-to-all-start.1 = ((f32[128,1,64]{2,1,0:T(1,128)}), f32[128,1,64]{2,1,0:T(1,128)S(1)}, u32[]{:S(2)}, u32[]{:S(2)}) async-start(f32[128,1,64]{2,1,0:T(1,128)} %copy.123), calls=%async_computation.1 | async-start | bytes 131072 | tf_op jit(solution)/shard_map/all_to_all | solution.py:90
